TPU v7x, 256 devices: a whole 4x4x8 slice. The times are simulated.
256 devices in a mesh: dp: 32 (over y_lo, z, core), expert: 8 (over y_hi, x).
Axes of the slice: x: 4, y: 4 (y_hi: 2, y_lo: 2; y = y_hi * 2 + y_lo), z: 8, core: 2. Of those that a mesh axis runs over, the one named last changes fastest.
Arguments:
- tokens: bfloat16 [65536, 2048], P(('dp', 'expert')), parts along dimension 0, may hold values from -6 to 6
- routes: int32 [65536, 2], P(('dp', 'expert')), parts along dimension 0, may hold values from 0 to 7, all different within a row; in each aligned block of 256 rows (0 to 255, 256 to 511, ...) at most 128 rows name the same one
- gate_values: bfloat16 [65536, 2], P(('dp', 'expert')), parts along dimension 0, may hold values from 0.099609375 to 1
- weight_in: bfloat16 [8, 2048, 1536], P('expert'), may hold values from -0.125 to 0.125
- weight_out: bfloat16 [8, 768, 2048], P('expert'), may hold values from -0.21875 to 0.21875
Outputs:
- mixed: bfloat16 [65536, 2048], P(('dp', 'expert')), parts along dimension 0
There are 32 independent parts, one for each index of `dp`. A program takes and returns all parts, laid end to end along the dimension named above; an argument that names none is the same for every part. Nothing has to cross between parts.
Inputs may be any that keep to these rules, and one draw needn't show every extreme that they name: `routes`: each row names 2 different experts. In each aligned block of 256 rows (the rows of one device) no expert is named by more than 128 rows, a bound that some block reaches.
All inputs are finite; a program needn't handle non-finite values.
Results may differ from a plain program's by a relative error of at most 0.012.
Values may be sent and summed in bfloat16 or wider, within the bound.
No kernel may reach another device: no remote copies, remote signals or barrier semaphores. Data moves between devices by JAX's collectives and lax.ppermute only.
A program may use at most 128 MiB of HBM per device.

v0:
```python
from functools import partial

import jax
import jax.numpy as jnp
from jax import lax
from jax.sharding import PartitionSpec as P


def assign_slots(route_block, gate_block, expert_id, capacity):
    count_rows = route_block.shape[0]
    matched = route_block == expert_id
    chosen = jnp.any(matched, axis=1)
    weights = jnp.sum(jnp.where(matched, gate_block.astype(jnp.float32), 0.0), axis=1)
    position = jnp.cumsum(chosen.astype(jnp.int32)) - 1
    target = jnp.where(chosen, position, capacity)
    slot_rows = (
        jnp.full((capacity,), count_rows, jnp.int32)
        .at[target]
        .set(jnp.arange(count_rows, dtype=jnp.int32), mode="drop")
    )
    is_used = slot_rows < count_rows
    clipped = jnp.minimum(slot_rows, count_rows - 1)
    slot_weight = jnp.where(is_used, weights[clipped], 0.0)
    return (slot_rows, clipped, slot_weight)


def expert_block(gathered_rows, slot_weight, w_first, w_second):
    width = gathered_rows.shape[-1]
    hidden_units = w_second.shape[0]
    flat_rows = gathered_rows.reshape(-1, width)
    projected = jnp.dot(flat_rows, w_first, preferred_element_type=jnp.float32)
    hidden = (jax.nn.silu(projected[:, :hidden_units]) * projected[:, hidden_units:]).astype(
        jnp.bfloat16
    )
    expert_out = jnp.dot(hidden, w_second, preferred_element_type=jnp.float32)
    contribution = (expert_out * slot_weight.reshape(-1, 1)).astype(jnp.bfloat16)
    return contribution.reshape(gathered_rows.shape)


def local(tokens, routes, gate_values, weight_in, weight_out):
    groups = lax.axis_size("expert")
    tok_rows = tokens.shape[0]
    width = tokens.shape[1]
    capacity = min(tok_rows, 2 * tok_rows * routes.shape[1] // groups)
    w_first = weight_in[0]
    w_second = weight_out[0]
    gathered, gates_all, routes_all = (
        lax.all_gather(tokens, "expert", axis=0, tiled=True),
        lax.all_gather(gate_values, "expert", axis=0, tiled=True),
        lax.all_gather(routes, "expert", axis=0, tiled=True),
    )
    my_expert = lax.axis_index("expert")
    gathered = gathered.reshape(groups, tok_rows, width)
    slot_rows, clipped, slot_weight = jax.vmap(
        partial(assign_slots, expert_id=my_expert, capacity=capacity)
    )(routes_all.reshape(groups, tok_rows, -1), gates_all.reshape(groups, tok_rows, -1))
    picked = jnp.take_along_axis(gathered, clipped[:, :, None], axis=1)
    contribution = expert_block(picked, slot_weight, w_first, w_second)
    sources = jnp.broadcast_to(jnp.arange(groups, dtype=jnp.int32)[:, None], slot_rows.shape)
    partial_out = (
        jnp.zeros((groups, tok_rows, width), jnp.float32)
        .at[sources, slot_rows]
        .add(contribution.astype(jnp.float32), mode="drop")
    )
    summed = lax.psum_scatter(
        partial_out.reshape(groups * tok_rows, width).astype(jnp.bfloat16),
        "expert",
        scatter_dimension=0,
        tiled=True,
    )
    return summed


def solution(mesh):
    in_specs = (
        P(("dp", "expert"), None),
        P(("dp", "expert"), None),
        P(("dp", "expert"), None),
        P("expert", None, None),
        P("expert", None, None),
    )
    out_specs = P(("dp", "expert"), None)
    return jax.shard_map(local, mesh=mesh, in_specs=in_specs, out_specs=out_specs, check_vma=False)
```

profile of v0, /device:TPU:38, one launch (start us, length us, event | category | flops | bytes accessed | tf_op | source)
XLA Modules:
  0.0 341.3 jit_solution(15728104457747690737)
XLA Ops:
  6.5 0.0 copy-start
  6.5 0.7 all-gather.2.cloned.1.call-update
  7.3 0.0 reduce-scatter.2.cloned.1.call-start
  7.3 28.6 %all_gather.9 = s32[2048,2]{0,1:T(2,128)S(1)} all-gather(s32[256,2]{0,1:T(2,128)} %param.6), channel_id=1, replica_groups=mesh['dp'=32,'expert'=8] {'expert'}, dimensions={0}, use_global_device_ids=true | all-gather | bytes 18432 | tf_op jit(solution)/shard_map/all_gather | solution.py:50
  36.0 19.4 %all_gather.11 = bf16[2048,2]{0,1:T(2,128)(2,1)S(1)} all-gather(bf16[256,2]{0,1:T(2,128)(2,1)} %param.7), channel_id=1, replica_groups=mesh['dp'=32,'expert'=8] {'expert'}, dimensions={0}, use_global_device_ids=true | all-gather | bytes 9216 | tf_op jit(solution)/shard_map/all_gather | solution.py:49
  55.5 0.6 reduce-window.6
  56.1 0.2 slice_reduce_fusion
  56.3 0.1 compare_select_fusion
  56.4 0.7 multiply_reduce_fusion
  57.1 0.7 and_reduce_fusion
  57.9 8.0 %scatter_custom_fusion = s32[1024]{0:T(1024)S(1)} fusion(s32[2048]{0:T(1024)S(1)} %bitcast.55, s32[2048]{0:T(1024)S(1)} %bitcast.54, s32[]{:T(128)} %constant.12.clone.1), kind=kCustom, calls=%fused_computation.39 | custom fusion | bytes 4100
  66.0 6.8 %gather_fusion.1 = f32[1024]{0:T(1024)S(1)} fusion(f32[8,256]{1,0:T(8,128)S(1)} %reduce_sum.12, s32[1024]{0:T(1024)S(1)} %fusion.11), kind=kCustom, calls=%fused_computation.1 | custom fusion | bytes 16384 | tf_op jit(solution)/shard_map/vmap()/gather | solution.py:23
  72.8 0.1 multiply_reduce_fusion.1
  72.8 0.0 copy-done.1
  72.8 0.1 and_reduce_fusion.1
  73.0 51.3 %all-gather.2.cloned.1.call-done = bf16[2048,2048]{1,0:T(8,128)(2,1)} async-done(((bf16[256,2048]{1,0:T(8,128)(2,1)}), bf16[2048,2048]{1,0:T(8,128)(2,1)}) %all-gather.2.cloned.1.call-update) | async-done | bytes 8388624 | tf_op jit(solution)/shard_map/all_gather | solution.py:48
  124.2 44.4 %gather_fusion = bf16[1024,2048]{1,0:T(8,128)(2,1)} fusion(bf16[8,256,2048]{2,1,0:T(8,128)(2,1)} %bitcast.50, s32[1024]{0:T(1024)S(1)} %fusion.11), kind=kCustom, calls=%fused_computation | custom fusion | bytes 8396800 | tf_op jit(solution)/shard_map/jit(take_along_axis)/gather | solution.py:57
  168.7 2.6 broadcast_select_fusion
  171.3 8.8 %fusion.3 = f32[1024,1536]{1,0:T(8,128)S(1)} fusion(bf16[1024,2048]{1,0:T(8,128)(2,1)S(1)} %bitcast.52, bf16[1,2048,1536]{2,1,0:T(8,128)(2,1)} %param.8), kind=kOutput, calls=%fused_computation.8 | convolution fusion | flops 6442450944 | bytes 16777216 | tf_op jit(solution)/shard_map/dot_general | solution.py:31
  180.1 5.1 %multiply_convert_fusion = bf16[1024,2048]{1,0:T(8,128)(2,1)} fusion(f32[1024]{0:T(1024)S(1)} %fusion.10, bf16[1,768,2048]{2,1,0:T(8,128)(2,1)S(1)} %copy-done, f32[1024,1536]{1,0:T(8,128)S(1)} %fusion.3), kind=kOutput, calls=%fused_computation.7 | convolution fusion | flops 3230138368 | bytes 13635584 | tf_op jit(solution)/shard_map/dot_general | solution.py:35
  185.2 21.5 %scatter_custom_fusion.1 = f32[2048,2048]{1,0:T(8,128)} fusion(s32[1024]{0:T(1024)S(1)} %select_bitcast_fusion.1, bf16[1024,2048]{1,0:T(8,128)(2,1)} %multiply_convert_fusion, f32[]{:T(128)} %constant.11.clone.1), kind=kCustom, calls=%fused_computation.4 | custom fusion | flops 4194304 | bytes 20971524
  206.7 9.1 %convert_element_type.40 = bf16[2048,2048]{1,0:T(8,128)(2,1)} convert(f32[2048,2048]{1,0:T(8,128)} %scatter_custom_fusion.1) | non-fusion elementwise | flops 4194304 | bytes 25165824 | tf_op jit(solution)/shard_map/convert_element_type | solution.py:66
  215.8 0.0 reduce-scatter.2.cloned.1.call-update
  215.8 118.6 %reduce-scatter.2.cloned.1.call-done = bf16[256,2048]{1,0:T(8,128)(2,1)} async-done(((bf16[2048,2048]{1,0:T(8,128)(2,1)}), bf16[256,2048]{1,0:T(8,128)(2,1)}) %reduce-scatter.2.cloned.1.call-update) | async-done | bytes 1048592 | tf_op jit(solution)/shard_map/reduce_scatter | solution.py:65
  (24 shorter events, 0.2 us)
Async XLA Ops:
  6.5 173.5 %copy-start = (bf16[1,768,2048]{2,1,0:T(8,128)(2,1)S(1)}, bf16[1,768,2048]{2,1,0:T(8,128)(2,1)}, u32[]{:S(2)}) copy-start(bf16[1,768,2048]{2,1,0:T(8,128)(2,1)} %param.9) | copy-start | bytes 9437188
  6.5 66.2 %copy-start.2 = (s32[2]{0:T(128)S(1)}, s32[2]{0:T(128)}, u32[]{:S(2)}) copy-start(s32[2]{0:T(128)} %constant.49) | copy-start | bytes 28
  6.5 66.3 %copy-start.1 = (s32[2]{0:T(128)S(1)}, s32[2]{0:T(128)}, u32[]{:S(2)}) copy-start(s32[2]{0:T(128)} %constant.52) | copy-start | bytes 28
  6.5 117.7 %all-gather.2.cloned.1.call-start = ((), (), s32[]{:S(2)}) async-start(), calls=%async_computation.1 | async-start | bytes 9437184 | tf_op jit(solution)/shard_map/all_gather | solution.py:48
  7.3 327.2 %reduce-scatter.2.cloned.1.call-start = ((), (), s32[]{:S(2)}) async-start(), calls=%async_computation.2 | async-start | bytes 9437184 | tf_op jit(solution)/shard_map/reduce_scatter | solution.py:65
Sparse Core Ops, SparseCore 0:
  10.0 114.2 all-gather.1
  215.9 118.4 reduce-scatter.1
where the time goes:
time: 344 us; the launch traced here: 341 us
  waiting for transfers between devices  171 us (50%)
  local copies, waits for them, and re-layouts  59.5 us (17%)
  blocking collectives  48 us (14%)
  other arithmetic  35.7 us (10%)
  matrix products  13.8 us (4%)
  between operations  13.6 us (4%)
    reduce_scatter x1, waiting for transfers between devices, local(): lax.psum_scatter(partial_out.reshape(groups * tok_rows, width).astype(jnp...  119 us
    all_gather x1, waiting for transfers between devices, local(): lax.all_gather(tokens, 'expert', axis=0, tiled=True)  51.3 us
    gather x1, local copies, waits for them, and re-layouts, local(): picked = jnp.take_along_axis(gathered, clipped[:, :, None], axis=1)  44.4 us
    all_gather x1, blocking collectives, local(): lax.all_gather(routes, 'expert', axis=0, tiled=True)  28.6 us
    unnamed x7, other arithmetic  23.2 us
    all_gather x1, blocking collectives, local(): lax.all_gather(gate_values, 'expert', axis=0, tiled=True)  19.4 us
    convert_element_type x1, other arithmetic, local(): partial_out.reshape(groups * tok_rows, width).astype(jnp.bfloat16)  9.08 us
    dot_general x1, matrix products, expert_block(): projected = jnp.dot(flat_rows, w_first, preferred_element_type=jnp.float32)  8.76 us
  transfers between devices with their start and end apart: 2, of which 2 were waited for; matrix products, arithmetic and copies ran while one was open for 5% of the time, Pallas kernels for 0%

commit v1 on v0

v1 whole, which is shorter than its diff:
```python
import jax
import jax.numpy as jnp
from jax import lax
from jax.sharding import PartitionSpec as P


def slot_matrix(routes, gate_values, groups, capacity):
    tok_rows = routes.shape[0]
    experts = jnp.arange(groups, dtype=jnp.int32)
    matched = routes[:, :, None] == experts[None, None, :]
    named = jnp.any(matched, axis=1)
    weight = jnp.sum(jnp.where(matched, gate_values.astype(jnp.float32)[:, :, None], 0.0), axis=1)
    position = jnp.cumsum(named.astype(jnp.int32), axis=0) - 1
    slots = jnp.arange(capacity, dtype=jnp.int32)
    picks = named.T[:, None, :] & (position.T[:, None, :] == slots[None, :, None])
    return picks.astype(jnp.bfloat16), weight.astype(jnp.bfloat16)


def local(tokens, routes, gate_values, weight_in, weight_out):
    groups = lax.axis_size("expert")
    tok_rows, width = tokens.shape
    capacity = min(tok_rows, 2 * tok_rows * routes.shape[1] // groups)
    hidden_units = weight_out.shape[1]
    me = lax.axis_index("expert")
    picks, weight = slot_matrix(routes, gate_values, groups, capacity)
    lanes = 128
    extended = jnp.concatenate(
        [tokens, jnp.pad(weight, ((0, 0), (0, lanes - groups)))], axis=1
    )
    outgoing = jnp.einsum(
        "ect,td->ecd", picks, extended, preferred_element_type=jnp.float32
    ).astype(jnp.bfloat16)
    incoming = lax.all_to_all(outgoing, "expert", 0, 0, tiled=True)
    rows = incoming[:, :, :width].reshape(groups * capacity, width)
    own = jnp.arange(groups, dtype=jnp.int32) == me
    gate = jnp.sum(
        jnp.where(own, incoming[:, :, width:width + groups].astype(jnp.float32), 0.0),
        axis=-1,
    ).reshape(-1, 1)
    projected = jnp.dot(rows, weight_in[0], preferred_element_type=jnp.float32)
    hidden = (jax.nn.silu(projected[:, :hidden_units]) * projected[:, hidden_units:]).astype(
        jnp.bfloat16
    )
    expert_out = jnp.dot(hidden, weight_out[0], preferred_element_type=jnp.float32)
    contribution = (expert_out * gate).astype(jnp.bfloat16).reshape(groups, capacity, width)
    returned = lax.all_to_all(contribution, "expert", 0, 0, tiled=True)
    mixed = jnp.einsum(
        "ect,ecd->td", picks, returned, preferred_element_type=jnp.float32
    )
    return mixed.astype(jnp.bfloat16)


def solution(mesh):
    in_specs = (
        P(("dp", "expert"), None),
        P(("dp", "expert"), None),
        P(("dp", "expert"), None),
        P("expert", None, None),
        P("expert", None, None),
    )
    out_specs = P(("dp", "expert"), None)
    return jax.shard_map(local, mesh=mesh, in_specs=in_specs, out_specs=out_specs, check_vma=False)
```

time: 344 us -> 155 us (0.45)
  waiting for transfers between devices: 171 us -> 65.1 us
  local copies, waits for them, and re-layouts: 59.5 us -> 4.38 us
  other arithmetic: 35.7 us -> 4.12 us
  between operations: 13.6 us -> 0.05 us
  starting transfers between devices: 0.04 us -> 7.4 us
  blocking collectives: 48 us -> 54.3 us
  matrix products: 13.8 us -> 18.1 us
    reduce_scatter x1 -> x0, waiting for transfers between devices: 119 us -> none  [local(): lax.psum_scatter(partial_out.reshape(groups * tok_rows, width).astype(jnp...]
    all_to_all x0 -> x1, waiting for transfers between devices: none -> 65.1 us  [local(): incoming = lax.all_to_all(outgoing, 'expert', 0, 0, tiled=True)]
    all_to_all x0 -> x1, blocking collectives: none -> 54.3 us  [local(): returned = lax.all_to_all(contribution, 'expert', 0, 0, tiled=True)]
    all_gather x1 -> x0, waiting for transfers between devices: 51.3 us -> none  [local(): lax.all_gather(tokens, 'expert', axis=0, tiled=True)]
    gather x2 -> x0, local copies, waits for them, and re-layouts: 51.2 us -> none  [the longest x1 44.4 us: local(): picked = jnp.take_along_axis(gathered, clipped[:, :, None], axis=1)]
    all_gather x2 -> x0, blocking collectives: 48 us -> none  [the longest x1 28.6 us: local(): lax.all_gather(routes, 'expert', axis=0, tiled=True)]
    unnamed x7 -> x0, other arithmetic: 23.2 us -> none
    convert_element_type x2 -> x1, other arithmetic: 9.08 us -> 0.8 us  [slot_matrix(): gate_values.astype(jnp.float32)[:, :, None]]
  transfers between devices with their start and end apart: 2 -> 1, of which waited for: 2 -> 1; matrix products, arithmetic and copies ran while one was open for 5% -> 0% of each run, Pallas kernels for 0% -> 0%
where the time goes in v1:
time: 155 us; the launch traced here: 153 us
  waiting for transfers between devices  65.1 us (42%)
  blocking collectives  54.3 us (35%)
  matrix products  18.1 us (12%)
  starting transfers between devices  7.4 us (5%)
  local copies, waits for them, and re-layouts  4.38 us (3%)
  other arithmetic  4.12 us (3%)
    all_to_all x1, waiting for transfers between devices, local(): incoming = lax.all_to_all(outgoing, 'expert', 0, 0, tiled=True)  65.1 us
    all_to_all x1, blocking collectives, local(): returned = lax.all_to_all(contribution, 'expert', 0, 0, tiled=True)  54.3 us
    all_to_all x1, starting transfers between devices, local(): incoming = lax.all_to_all(outgoing, 'expert', 0, 0, tiled=True)  7.4 us
    dot_general x1, matrix products, local(): projected = jnp.dot(rows, weight_in[0], preferred_element_type=jnp.float32)  6.65 us
    dot_general x1, matrix products, local(): jnp.einsum('ect,td->ecd', picks, extended, preferred_element_type=jnp.flo...  4.99 us
    dot_general x1, matrix products, local(): jnp.dot(hidden, weight_out[0], preferred_element_type=jnp.float32)  3.78 us
  transfers between devices with their start and end apart: 1, of which 1 were waited for; matrix products, arithmetic and copies ran while one was open for 0% of the time, Pallas kernels for 0%

profile of v1, /device:TPU:38, one launch (start us, length us, event | category | flops | bytes accessed | tf_op | source)
XLA Modules:
  0.0 153.5 jit_solution(10196206741956601339)
XLA Ops:
  0.0 0.0 copy-start
  0.0 0.8 fusion.22
  0.8 0.8 convert_element_type.26
  1.6 0.7 select_reduce_fusion.1
  2.3 0.6 reduce-window.6
  2.9 0.2 slice_reduce_fusion
  3.2 0.1 add_bitcast_fusion
  3.2 0.1 copy.17
  3.4 5.0 %convolution_convert_fusion = bf16[8,128,2176]{2,1,0:T(8,128)(2,1)} fusion(bf16[256,8]{1,0:T(8,128)(2,1)S(1)} %copy.17, bf16[256,2048]{1,0:T(8,128)(2,1)} %param.5, s32[8,256]{1,0:T(8,128)S(1)} %add_bitcast_fusion, pred[8,256]{1,0:T(8,128)(4,1)S(1)} %bitcast.26), kind=kOutput, calls=%fused_computation.3 | convolution fusion | flops 1146945536 | bytes 5519360 | tf_op jit(solution)/shard_map/ect,td->ecd/dot_general | solution.py:30
  8.4 7.4 %all-to-all-start = ((bf16[8,128,2176]{2,1,0:T(8,128)(2,1)}), bf16[8,128,2176]{2,1,0:T(8,128)(2,1)}, u32[]{:S(2)}, u32[]{:S(2)}) async-start(bf16[8,128,2176]{2,1,0:T(8,128)(2,1)} %convolution_convert_fusion), calls=%async_computation | async-start | bytes 8912896 | tf_op jit(solution)/shard_map/all_to_all | solution.py:33
  15.8 65.1 %all-to-all-done = bf16[8,128,2176]{2,1,0:T(8,128)(2,1)} async-done(((bf16[8,128,2176]{2,1,0:T(8,128)(2,1)}), bf16[8,128,2176]{2,1,0:T(8,128)(2,1)}, u32[]{:S(2)}, u32[]{:S(2)}) %all-to-all-start) | async-done | bytes 4456480 | tf_op jit(solution)/shard_map/all_to_all | solution.py:33
  80.9 0.0 copy-start.1
  80.9 2.7 %slice.25 = bf16[8,128,2048]{2,1,0:T(8,128)(2,1)S(1)} slice(bf16[8,128,2176]{2,1,0:T(8,128)(2,1)} %all-to-all-done), slice={[0:8], [0:128], [0:2048]} | slice | bytes 8388608 | tf_op jit(solution)/shard_map/slice | solution.py:34
  83.6 1.4 copy-done.1
  85.0 6.6 %fusion = f32[1024,1536]{1,0:T(8,128)S(1)} fusion(bf16[1024,2048]{1,0:T(8,128)(2,1)S(1)} %bitcast.25, bf16[1,2048,1536]{2,1,0:T(8,128)(2,1)S(1)} %copy-done.1), kind=kOutput, calls=%fused_computation.1 | convolution fusion | flops 6442450944 | bytes 16777216 | tf_op jit(solution)/shard_map/dot_general | solution.py:40
  91.6 1.1 select_reduce_fusion
  92.7 0.0 copy-done
  92.7 3.8 %multiply_convert_fusion = bf16[1024,2048]{1,0:T(8,128)(2,1)S(1)} fusion(f32[1024]{0:T(1024)S(1)} %bitcast.28, bf16[1,768,2048]{2,1,0:T(8,128)(2,1)S(1)} %copy-done, f32[1024,1536]{1,0:T(8,128)S(1)} %fusion), kind=kOutput, calls=%fused_computation | convolution fusion | flops 3230138368 | bytes 13635584 | tf_op jit(solution)/shard_map/dot_general | solution.py:44
  96.5 54.3 %all_to_all.10 = bf16[8,128,2048]{2,1,0:T(8,128)(2,1)S(1)} all-to-all(bf16[8,128,2048]{2,1,0:T(8,128)(2,1)S(1)} %bitcast.24), channel_id=1, replica_groups=mesh['dp'=32,'expert'=8] {'expert'}, dimensions={0} | all-to-all | bytes 8388608 | tf_op jit(solution)/shard_map/all_to_all | solution.py:46
  150.8 2.6 %fusion.4 = bf16[256,2048]{1,0:T(8,128)(2,1)} fusion(bf16[8,128,2048]{2,1,0:T(8,128)(2,1)S(1)} %all_to_all.10, s32[8,256]{1,0:T(8,128)S(1)} %add_bitcast_fusion, pred[8,256]{1,0:T(8,128)(4,1)S(1)} %bitcast.27), kind=kOutput, calls=%fused_computation.8 | convolution fusion | flops 1074790400 | bytes 5253120 | tf_op jit(solution)/shard_map/ect,ecd->td/dot_general | solution.py:47
  (4 shorter events, 0.1 us)
Async XLA Ops:
  0.0 92.7 %copy-start = (bf16[1,768,2048]{2,1,0:T(8,128)(2,1)S(1)}, bf16[1,768,2048]{2,1,0:T(8,128)(2,1)}, u32[]{:S(2)}) copy-start(bf16[1,768,2048]{2,1,0:T(8,128)(2,1)} %param.9) | copy-start | bytes 9437188
  8.4 72.6 %all-to-all-start = ((bf16[8,128,2176]{2,1,0:T(8,128)(2,1)}), bf16[8,128,2176]{2,1,0:T(8,128)(2,1)}, u32[]{:S(2)}, u32[]{:S(2)}) async-start(bf16[8,128,2176]{2,1,0:T(8,128)(2,1)} %convolution_convert_fusion), calls=%async_computation | async-start | bytes 8912896 | tf_op jit(solution)/shard_map/all_to_all | solution.py:33
  80.9 4.0 %copy-start.1 = (bf16[1,2048,1536]{2,1,0:T(8,128)(2,1)S(1)}, bf16[1,2048,1536]{2,1,0:T(8,128)(2,1)}, u32[]{:S(2)}) copy-start(bf16[1,2048,1536]{2,1,0:T(8,128)(2,1)} %param.8) | copy-start | bytes 18874372

commit v2 on v1

v2 whole, which is shorter than its diff:
```python
import jax
import jax.numpy as jnp
from jax import lax
from jax.sharding import PartitionSpec as P


def slot_matrices(routes, gate_values, groups, capacity):
    experts = jnp.arange(groups, dtype=jnp.int32)
    matched = routes[:, :, None] == experts[None, None, :]
    named = jnp.any(matched, axis=1)
    weight = jnp.sum(jnp.where(matched, gate_values.astype(jnp.float32)[:, :, None], 0.0), axis=1)
    position = jnp.cumsum(named.astype(jnp.int32), axis=0) - 1
    slots = jnp.arange(capacity, dtype=jnp.int32)
    picks = named.T[:, None, :] & (position.T[:, None, :] == slots[None, :, None])
    weighted = jnp.where(picks, weight.T[:, None, :], 0.0)
    return picks.astype(jnp.bfloat16), weighted.astype(jnp.bfloat16)


def local(tokens, routes, gate_values, weight_in, weight_out):
    groups = lax.axis_size("expert")
    tok_rows, width = tokens.shape
    capacity = min(tok_rows, 2 * tok_rows * routes.shape[1] // groups)
    hidden_units = weight_out.shape[1]
    picks, weighted = slot_matrices(routes, gate_values, groups, capacity)
    outgoing = jnp.einsum(
        "ect,td->ecd", picks, tokens, preferred_element_type=jnp.float32
    ).astype(jnp.bfloat16)
    incoming = lax.all_to_all(outgoing, "expert", 0, 0, tiled=True)
    rows = incoming.reshape(groups * capacity, width)
    projected = jnp.dot(rows, weight_in[0], preferred_element_type=jnp.float32)
    hidden = (jax.nn.silu(projected[:, :hidden_units]) * projected[:, hidden_units:]).astype(
        jnp.bfloat16
    )
    expert_out = jnp.dot(hidden, weight_out[0], preferred_element_type=jnp.float32)
    expert_out = expert_out.astype(jnp.bfloat16).reshape(groups, capacity, width)
    returned = lax.all_to_all(expert_out, "expert", 0, 0, tiled=True)
    mixed = jnp.einsum(
        "ect,ecd->td", weighted, returned, preferred_element_type=jnp.float32
    )
    return mixed.astype(jnp.bfloat16)


def solution(mesh):
    in_specs = (
        P(("dp", "expert"), None),
        P(("dp", "expert"), None),
        P(("dp", "expert"), None),
        P("expert", None, None),
        P("expert", None, None),
    )
    out_specs = P(("dp", "expert"), None)
    return jax.shard_map(local, mesh=mesh, in_specs=in_specs, out_specs=out_specs, check_vma=False)
```

time: 155 us -> 142 us (0.916); the launches traced: 153 us -> 142 us
  waiting for transfers between devices: 65.1 us -> 57.1 us
  local copies, waits for them, and re-layouts: 4.38 us -> 0.24 us
  other arithmetic: 4.12 us -> 1.54 us
  blocking collectives: 54.3 us -> 56.7 us
  matrix products: 18.1 us -> 20.3 us
    all_to_all x1, waiting for transfers between devices: 65.1 us -> 57.1 us  [local(): returned = lax.all_to_all(expert_out, 'expert', 0, 0, tiled=True)]
    slice x2 -> x1, local copies, waits for them, and re-layouts: 2.87 us -> 0.21 us  [the longest x1 2.65 us: local(): rows = incoming[:, :, :width].reshape(groups * capacity, width)]
    all_to_all x1, blocking collectives: 54.3 us -> 56.7 us  [local(): incoming = lax.all_to_all(outgoing, 'expert', 0, 0, tiled=True)]
    reduce_sum x2 -> x1, other arithmetic: 1.78 us -> 0.01 us  [slot_matrices(): jnp.sum(jnp.where(matched, gate_values.astype(jnp.float32)[:, :, None], 0...]
where the time goes in v2:
time: 142 us
  waiting for transfers between devices  57.1 us (40%)
  blocking collectives  56.7 us (40%)
  matrix products  20.3 us (14%)
  starting transfers between devices  6.29 us (4%)
  other arithmetic  1.54 us (1%)
    all_to_all x1, waiting for transfers between devices, local(): returned = lax.all_to_all(expert_out, 'expert', 0, 0, tiled=True)  57.1 us
    all_to_all x1, blocking collectives, local(): incoming = lax.all_to_all(outgoing, 'expert', 0, 0, tiled=True)  56.7 us
    dot_general x1, matrix products, local(): projected = jnp.dot(rows, weight_in[0], preferred_element_type=jnp.float32)  6.64 us
    all_to_all x1, starting transfers between devices, local(): returned = lax.all_to_all(expert_out, 'expert', 0, 0, tiled=True)  6.29 us
    dot_general x1, matrix products, local(): jnp.dot(hidden, weight_out[0], preferred_element_type=jnp.float32)  5.08 us
    dot_general x1, matrix products, local(): jnp.einsum('ect,ecd->td', weighted, returned, preferred_element_type=jnp....  5.05 us
    dot_general x1, matrix products, local(): jnp.einsum('ect,td->ecd', picks, tokens, preferred_element_type=jnp.float32)  3.5 us
  transfers between devices with their start and end apart: 1, of which 1 were waited for; matrix products, arithmetic and copies ran while one was open for 0% of the time, Pallas kernels for 0%

profile of v2, /device:TPU:38, one launch (start us, length us, event | category | flops | bytes accessed | tf_op | source)
XLA Modules:
  0.0 142.2 jit_solution(5394476376949914468)
XLA Ops:
  0.0 0.0 copy-start
  0.0 0.8 fusion.16
  0.8 0.6 reduce-window.6
  1.4 0.2 slice_reduce_fusion
  1.7 0.1 add_bitcast_fusion
  1.8 0.0 slice-start
  1.8 3.5 %convolution_convert_fusion = bf16[8,128,2048]{2,1,0:T(8,128)(2,1)S(1)} fusion(bf16[256,2048]{1,0:T(8,128)(2,1)} %param.5, s32[8,256]{1,0:T(8,128)S(1)} %add_bitcast_fusion, pred[8,256]{1,0:T(8,128)(4,1)S(1)} %bitcast.26), kind=kOutput, calls=%fused_computation.2 | convolution fusion | flops 1076363264 | bytes 5253120 | tf_op jit(solution)/shard_map/ect,td->ecd/dot_general | solution.py:25
  5.3 0.0 slice-start.1
  5.3 56.7 %all_to_all.10 = bf16[8,128,2048]{2,1,0:T(8,128)(2,1)S(1)} all-to-all(bf16[8,128,2048]{2,1,0:T(8,128)(2,1)S(1)} %convolution_convert_fusion), channel_id=1, replica_groups=mesh['dp'=32,'expert'=8] {'expert'}, dimensions={0} | all-to-all | bytes 8388608 | tf_op jit(solution)/shard_map/all_to_all | solution.py:28
  62.0 0.0 slice-done
  62.0 0.0 slice-done.1
  62.0 6.6 %fusion = f32[1024,1536]{1,0:T(8,128)S(1)} fusion(bf16[1024,2048]{1,0:T(8,128)(2,1)S(1)} %bitcast.25, bf16[1,2048,1536]{2,1,0:T(8,128)(2,1)S(1)} %bitcast.30), kind=kOutput, calls=%fused_computation | convolution fusion | flops 6442450944 | bytes 16777216 | tf_op jit(solution)/shard_map/dot_general | solution.py:30
  68.7 0.0 copy-done
  68.7 5.1 %convolution_convert_fusion.1 = bf16[1024,2048]{1,0:T(8,128)(2,1)} fusion(bf16[1,768,2048]{2,1,0:T(8,128)(2,1)S(1)} %copy-done, f32[1024,1536]{1,0:T(8,128)S(1)} %fusion), kind=kOutput, calls=%fused_computation.3 | convolution fusion | flops 3228041216 | bytes 13631488 | tf_op jit(solution)/shard_map/dot_general | solution.py:34
  73.7 0.0 copy-start.2
  73.7 0.0 copy-start.1
  73.7 6.3 %all-to-all-start.1 = ((bf16[8,128,2048]{2,1,0:T(8,128)(2,1)}), bf16[8,128,2048]{2,1,0:T(8,128)(2,1)}, u32[]{:S(2)}, u32[]{:S(2)}) async-start(bf16[8,128,2048]{2,1,0:T(8,128)(2,1)} %bitcast.24), calls=%async_computation.1 | async-start | bytes 8388608 | tf_op jit(solution)/shard_map/all_to_all | solution.py:36
  80.0 0.0 copy-done.2
  80.0 0.0 copy-done.1
  80.1 57.1 %all-to-all-done.1 = bf16[8,128,2048]{2,1,0:T(8,128)(2,1)} async-done(((bf16[8,128,2048]{2,1,0:T(8,128)(2,1)}), bf16[8,128,2048]{2,1,0:T(8,128)(2,1)}, u32[]{:S(2)}, u32[]{:S(2)}) %all-to-all-start.1) | async-done | bytes 4194336 | tf_op jit(solution)/shard_map/all_to_all | solution.py:36
  137.2 5.1 %fusion.4 = bf16[256,2048]{1,0:T(8,128)(2,1)} fusion(bf16[8,128,2048]{2,1,0:T(8,128)(2,1)} %all-to-all-done.1, bf16[8,256]{1,0:T(8,128)(2,1)S(1)} %bitcast.28, s32[8,256]{1,0:T(8,128)S(1)} %add_bitcast_fusion, pred[8,256]{1,0:T(8,128)(4,1)S(1)} %bitcast.27), kind=kOutput, calls=%fused_computation.8 | convolution fusion | flops 1075052544 | bytes 5257216 | tf_op jit(solution)/shard_map/ect,ecd->td/dot_general | solution.py:37
  (6 shorter events, 0.1 us)
Async XLA Ops:
  0.0 68.7 %copy-start = (bf16[1,768,2048]{2,1,0:T(8,128)(2,1)S(1)}, bf16[1,768,2048]{2,1,0:T(8,128)(2,1)}, u32[]{:S(2)}) copy-start(bf16[1,768,2048]{2,1,0:T(8,128)(2,1)} %param.9) | copy-start | bytes 9437188
  1.8 60.3 %slice-start = ((s8[6291456]{0:T(1024)(128)(4,1)}), s8[4194304]{0:T(1024)(128)(4,1)S(1)}, s32[]{:S(2)}) async-start(s8[6291456]{0:T(1024)(128)(4,1)} %bitcast.29), calls=%async_computation.2 | async-start | bytes 8388608
  5.3 56.7 %slice-start.1 = ((s8[6291456]{0:T(1024)(128)(4,1)}), s8[2097152]{0:T(1024)(128)(4,1)S(1)}, s32[]{:S(2)}) async-start(s8[6291456]{0:T(1024)(128)(4,1)} %bitcast.29), calls=%async_computation.3 | async-start | bytes 4194304
  73.7 6.3 %copy-start.2 = (bf16[256,2]{0,1:T(2,128)(2,1)S(1)}, bf16[256,2]{0,1:T(2,128)(2,1)}, u32[]{:S(2)}) copy-start(bf16[256,2]{0,1:T(2,128)(2,1)} %param.7) | copy-start | bytes 3076
  73.7 6.3 %copy-start.1 = (s32[256,2]{0,1:T(2,128)S(1)}, s32[256,2]{0,1:T(2,128)}, u32[]{:S(2)}) copy-start(s32[256,2]{0,1:T(2,128)} %param.6) | copy-start | bytes 6148
  73.7 63.4 %all-to-all-start.1 = ((bf16[8,128,2048]{2,1,0:T(8,128)(2,1)}), bf16[8,128,2048]{2,1,0:T(8,128)(2,1)}, u32[]{:S(2)}, u32[]{:S(2)}) async-start(bf16[8,128,2048]{2,1,0:T(8,128)(2,1)} %bitcast.24), calls=%async_computation.1 | async-start | bytes 8388608 | tf_op jit(solution)/shard_map/all_to_all | solution.py:36

commit v3 on v2

v3 whole, which is shorter than its diff:
```python
import jax
import jax.numpy as jnp
from jax import lax
from jax.sharding import PartitionSpec as P

CHUNKS = 2


def slot_matrices(routes, gate_values, groups, capacity):
    experts = jnp.arange(groups, dtype=jnp.int32)
    matched = routes[:, :, None] == experts[None, None, :]
    named = jnp.any(matched, axis=1)
    weight = jnp.sum(jnp.where(matched, gate_values.astype(jnp.float32)[:, :, None], 0.0), axis=1)
    position = jnp.cumsum(named.astype(jnp.int32), axis=0) - 1
    slots = jnp.arange(capacity, dtype=jnp.int32)
    picks = named.T[:, None, :] & (position.T[:, None, :] == slots[None, :, None])
    weighted = jnp.where(picks, weight.T[:, None, :], 0.0)
    return picks.astype(jnp.bfloat16), weighted.astype(jnp.bfloat16)


def expert_rows(rows, w_first, w_second):
    hidden_units = w_second.shape[0]
    projected = jnp.dot(rows, w_first, preferred_element_type=jnp.float32)
    hidden = (jax.nn.silu(projected[:, :hidden_units]) * projected[:, hidden_units:]).astype(
        jnp.bfloat16
    )
    return jnp.dot(hidden, w_second, preferred_element_type=jnp.float32).astype(jnp.bfloat16)


def local(tokens, routes, gate_values, weight_in, weight_out):
    groups = lax.axis_size("expert")
    tok_rows, width = tokens.shape
    capacity = min(tok_rows, 2 * tok_rows * routes.shape[1] // groups)
    picks, weighted = slot_matrices(routes, gate_values, groups, capacity)
    step = capacity // CHUNKS
    mixed = None
    for k in range(CHUNKS):
        with jax.named_scope(f"chunk{k}"):
            part = slice(k * step, (k + 1) * step)
            outgoing = jnp.einsum(
                "ect,td->ecd", picks[:, part], tokens, preferred_element_type=jnp.float32
            ).astype(jnp.bfloat16)
            incoming = lax.all_to_all(outgoing, "expert", 0, 0, tiled=True)
            done = expert_rows(incoming.reshape(groups * step, width), weight_in[0], weight_out[0])
            returned = lax.all_to_all(done.reshape(groups, step, width), "expert", 0, 0, tiled=True)
            share = jnp.einsum(
                "ect,ecd->td", weighted[:, part], returned, preferred_element_type=jnp.float32
            )
            mixed = share if mixed is None else mixed + share
    return mixed.astype(jnp.bfloat16)


def solution(mesh):
    in_specs = (
        P(("dp", "expert"), None),
        P(("dp", "expert"), None),
        P(("dp", "expert"), None),
        P("expert", None, None),
        P("expert", None, None),
    )
    out_specs = P(("dp", "expert"), None)
    return jax.shard_map(local, mesh=mesh, in_specs=in_specs, out_specs=out_specs, check_vma=False)
```

time: 142 us -> 147 us (1.035)
  the two profiles are of different devices: /device:TPU:38 before, /device:TPU:1 now
where the time goes in v3:
time: 147 us; the launch traced here: 146 us
  waiting for transfers between devices  87.9 us (60%)
  matrix products  33 us (22%)
  starting transfers between devices  22.2 us (15%)
  other arithmetic  2 us (1%)
    all_to_all x2, waiting for transfers between devices, local(): incoming = lax.all_to_all(outgoing, 'expert', 0, 0, tiled=True)  44.7 us
    all_to_all x2, waiting for transfers between devices, local(): lax.all_to_all(done.reshape(groups, step, width), 'expert', 0, 0, tiled=T...  43.2 us
    dot_general x2, matrix products, expert_rows(): projected = jnp.dot(rows, w_first, preferred_element_type=jnp.float32)  12.3 us
    all_to_all x2, starting transfers between devices, local(): incoming = lax.all_to_all(outgoing, 'expert', 0, 0, tiled=True)  12.2 us
    all_to_all x2, starting transfers between devices, local(): lax.all_to_all(done.reshape(groups, step, width), 'expert', 0, 0, tiled=T...  10 us
    dot_general x2, matrix products, local(): jnp.einsum('ect,ecd->td', weighted[:, part], returned, preferred_element_...  7.69 us
    dot_general x2, matrix products, local(): jnp.einsum('ect,td->ecd', picks[:, part], tokens, preferred_element_type=...  6.61 us
    dot_general x2, matrix products, expert_rows(): jnp.dot(hidden, w_second, preferred_element_type=jnp.float32)  6.33 us
  transfers between devices with their start and end apart: 4, of which 4 were waited for; matrix products, arithmetic and copies ran while one was open for 18% of the time, Pallas kernels for 0%

profile of v3, /device:TPU:1, one launch (start us, length us, event | category | flops | bytes accessed | tf_op | source)
XLA Modules:
  0.0 146.2 jit_solution(2478689354773993253)
XLA Ops:
  0.0 0.8 fusion.29
  0.8 0.6 reduce-window.6
  1.4 0.2 slice_reduce_fusion
  1.7 0.1 add_bitcast_fusion
  1.8 0.2 fusion.20
  1.9 3.3 %convolution_convert_fusion = bf16[8,64,2048]{2,1,0:T(8,128)(2,1)} fusion(bf16[256,2048]{1,0:T(8,128)(2,1)} %param.5, pred[8,128,256]{2,1,0:T(32,128)(4,1)S(1)} %fusion.20), kind=kOutput, calls=%fused_computation.8 | convolution fusion | flops 537919488 | bytes 3276800 | tf_op jit(solution)/shard_map/chunk1/ect,td->ecd/dot_general | solution.py:40
  5.2 7.5 %all-to-all-start.2 = ((bf16[8,64,2048]{2,1,0:T(8,128)(2,1)}), bf16[8,64,2048]{2,1,0:T(8,128)(2,1)}, u32[]{:S(2)}, u32[]{:S(2)}) async-start(bf16[8,64,2048]{2,1,0:T(8,128)(2,1)} %convolution_convert_fusion), calls=%async_computation.2 | async-start | bytes 4194304 | tf_op jit(solution)/shard_map/chunk1/all_to_all | solution.py:43
  12.7 3.3 %convolution_convert_fusion.1 = bf16[8,64,2048]{2,1,0:T(8,128)(2,1)} fusion(bf16[256,2048]{1,0:T(8,128)(2,1)} %param.5, pred[8,128,256]{2,1,0:T(32,128)(4,1)S(1)} %fusion.20), kind=kOutput, calls=%fused_computation.9 | convolution fusion | flops 537919488 | bytes 3276800 | tf_op jit(solution)/shard_map/chunk0/ect,td->ecd/dot_general | solution.py:40
  16.0 25.4 %all-to-all-done.2 = bf16[8,64,2048]{2,1,0:T(8,128)(2,1)} async-done(((bf16[8,64,2048]{2,1,0:T(8,128)(2,1)}), bf16[8,64,2048]{2,1,0:T(8,128)(2,1)}, u32[]{:S(2)}, u32[]{:S(2)}) %all-to-all-start.2) | async-done | bytes 2097184 | tf_op jit(solution)/shard_map/chunk1/all_to_all | solution.py:43
  41.4 4.7 %all-to-all-start = ((bf16[8,64,2048]{2,1,0:T(8,128)(2,1)}), bf16[8,64,2048]{2,1,0:T(8,128)(2,1)}, u32[]{:S(2)}, u32[]{:S(2)}) async-start(bf16[8,64,2048]{2,1,0:T(8,128)(2,1)} %convolution_convert_fusion.1), calls=%async_computation | async-start | bytes 4194304 | tf_op jit(solution)/shard_map/chunk0/all_to_all | solution.py:43
  46.1 6.2 %fusion = f32[512,1536]{1,0:T(8,128)S(1)} fusion(bf16[512,2048]{1,0:T(8,128)(2,1)} %bitcast.10, bf16[1,2048,1536]{2,1,0:T(8,128)(2,1)} %param.8), kind=kOutput, calls=%fused_computation | convolution fusion | flops 3221225472 | bytes 11534336 | tf_op jit(solution)/shard_map/chunk1/dot_general | solution.py:23
  52.3 3.2 %fusion.11 = bf16[512,2048]{1,0:T(8,128)(2,1)} fusion(bf16[1,768,2048]{2,1,0:T(8,128)(2,1)S(1)} %copy-done, f32[512,1536]{1,0:T(8,128)S(1)} %fusion), kind=kOutput, calls=%fused_computation.11 | convolution fusion | flops 1614020608 | bytes 8388608 | tf_op jit(solution)/shard_map/chunk1/dot_general | solution.py:27
  55.5 19.3 %all-to-all-done = bf16[8,64,2048]{2,1,0:T(8,128)(2,1)} async-done(((bf16[8,64,2048]{2,1,0:T(8,128)(2,1)}), bf16[8,64,2048]{2,1,0:T(8,128)(2,1)}, u32[]{:S(2)}, u32[]{:S(2)}) %all-to-all-start) | async-done | bytes 2097184 | tf_op jit(solution)/shard_map/chunk0/all_to_all | solution.py:43
  74.8 4.3 %all-to-all-start.3 = ((bf16[8,64,2048]{2,1,0:T(8,128)(2,1)}), bf16[8,64,2048]{2,1,0:T(8,128)(2,1)}, u32[]{:S(2)}, u32[]{:S(2)}) async-start(bf16[8,64,2048]{2,1,0:T(8,128)(2,1)} %bitcast.43), calls=%async_computation.3 | async-start | bytes 4194304 | tf_op jit(solution)/shard_map/chunk1/all_to_all | solution.py:45
  79.2 6.2 %fusion.2 = f32[512,1536]{1,0:T(8,128)S(1)} fusion(bf16[512,2048]{1,0:T(8,128)(2,1)} %bitcast.5, bf16[1,2048,1536]{2,1,0:T(8,128)(2,1)} %param.8), kind=kOutput, calls=%fused_computation.2 | convolution fusion | flops 3221225472 | bytes 11534336 | tf_op jit(solution)/shard_map/chunk0/dot_general | solution.py:23
  85.3 3.1 %fusion.8 = bf16[512,2048]{1,0:T(8,128)(2,1)} fusion(bf16[1,768,2048]{2,1,0:T(8,128)(2,1)S(1)} %copy-done, f32[512,1536]{1,0:T(8,128)S(1)} %fusion.2), kind=kOutput, calls=%fused_computation.10 | convolution fusion | flops 1614020608 | bytes 8388608 | tf_op jit(solution)/shard_map/chunk0/dot_general | solution.py:27
  88.5 19.3 %all-to-all-done.3 = bf16[8,64,2048]{2,1,0:T(8,128)(2,1)} async-done(((bf16[8,64,2048]{2,1,0:T(8,128)(2,1)}), bf16[8,64,2048]{2,1,0:T(8,128)(2,1)}, u32[]{:S(2)}, u32[]{:S(2)}) %all-to-all-start.3) | async-done | bytes 2097184 | tf_op jit(solution)/shard_map/chunk1/all_to_all | solution.py:45
  107.8 5.7 %all-to-all-start.1 = ((bf16[8,64,2048]{2,1,0:T(8,128)(2,1)}), bf16[8,64,2048]{2,1,0:T(8,128)(2,1)}, u32[]{:S(2)}, u32[]{:S(2)}) async-start(bf16[8,64,2048]{2,1,0:T(8,128)(2,1)} %bitcast.42), calls=%async_computation.1 | async-start | bytes 4194304 | tf_op jit(solution)/shard_map/chunk0/all_to_all | solution.py:45
  113.4 0.0 copy-done.3
  113.5 0.3 select_convert_fusion
  113.8 0.8 copy-done.1
  114.6 3.7 %convolution_bitcast_fusion = f32[256,2048]{1,0:T(8,128)} fusion(bf16[8,64,2048]{2,1,0:T(8,128)(2,1)} %all-to-all-done.3, bf16[8,128,256]{2,1,0:T(8,128)(2,1)S(1)} %select_convert_fusion), kind=kOutput, calls=%fused_computation.12 | convolution fusion | flops 536870912 | bytes 4456448 | tf_op jit(solution)/shard_map/chunk1/ect,ecd->td/dot_general | solution.py:46
  118.3 23.9 %all-to-all-done.1 = bf16[8,64,2048]{2,1,0:T(8,128)(2,1)} async-done(((bf16[8,64,2048]{2,1,0:T(8,128)(2,1)}), bf16[8,64,2048]{2,1,0:T(8,128)(2,1)}, u32[]{:S(2)}, u32[]{:S(2)}) %all-to-all-start.1) | async-done | bytes 2097184 | tf_op jit(solution)/shard_map/chunk0/all_to_all | solution.py:45
  142.2 4.0 %fusion.15 = bf16[256,2048]{1,0:T(8,128)(2,1)} fusion(f32[256,2048]{1,0:T(8,128)} %convolution_bitcast_fusion, bf16[8,64,2048]{2,1,0:T(8,128)(2,1)} %all-to-all-done.1, bf16[8,128,256]{2,1,0:T(8,128)(2,1)} %copy-done.1), kind=kOutput, calls=%fused_computation.15 | convolution fusion | flops 537919488 | bytes 5505024 | tf_op jit(solution)/shard_map/chunk0/ect,ecd->td/dot_general | solution.py:46
  (11 shorter events, 0.1 us)
Async XLA Ops:
  0.0 52.3 %copy-start = (bf16[1,768,2048]{2,1,0:T(8,128)(2,1)S(1)}, bf16[1,768,2048]{2,1,0:T(8,128)(2,1)}, u32[]{:S(2)}) copy-start(bf16[1,768,2048]{2,1,0:T(8,128)(2,1)} %param.9) | copy-start | bytes 9437188
  5.2 36.2 %all-to-all-start.2 = ((bf16[8,64,2048]{2,1,0:T(8,128)(2,1)}), bf16[8,64,2048]{2,1,0:T(8,128)(2,1)}, u32[]{:S(2)}, u32[]{:S(2)}) async-start(bf16[8,64,2048]{2,1,0:T(8,128)(2,1)} %convolution_convert_fusion), calls=%async_computation.2 | async-start | bytes 4194304 | tf_op jit(solution)/shard_map/chunk1/all_to_all | solution.py:43
  41.4 33.4 %all-to-all-start = ((bf16[8,64,2048]{2,1,0:T(8,128)(2,1)}), bf16[8,64,2048]{2,1,0:T(8,128)(2,1)}, u32[]{:S(2)}, u32[]{:S(2)}) async-start(bf16[8,64,2048]{2,1,0:T(8,128)(2,1)} %convolution_convert_fusion.1), calls=%async_computation | async-start | bytes 4194304 | tf_op jit(solution)/shard_map/chunk0/all_to_all | solution.py:43
  74.8 33.0 %all-to-all-start.3 = ((bf16[8,64,2048]{2,1,0:T(8,128)(2,1)}), bf16[8,64,2048]{2,1,0:T(8,128)(2,1)}, u32[]{:S(2)}, u32[]{:S(2)}) async-start(bf16[8,64,2048]{2,1,0:T(8,128)(2,1)} %bitcast.43), calls=%async_computation.3 | async-start | bytes 4194304 | tf_op jit(solution)/shard_map/chunk1/all_to_all | solution.py:45
  107.8 5.7 %copy-start.3 = (bf16[256,2]{0,1:T(2,128)(2,1)S(1)}, bf16[256,2]{0,1:T(2,128)(2,1)}, u32[]{:S(2)}) copy-start(bf16[256,2]{0,1:T(2,128)(2,1)} %param.7) | copy-start | bytes 3076
  107.8 5.7 %copy-start.2 = (s32[256,2]{0,1:T(2,128)S(1)}, s32[256,2]{0,1:T(2,128)}, u32[]{:S(2)}) copy-start(s32[256,2]{0,1:T(2,128)} %param.6) | copy-start | bytes 6148
  107.8 34.4 %all-to-all-start.1 = ((bf16[8,64,2048]{2,1,0:T(8,128)(2,1)}), bf16[8,64,2048]{2,1,0:T(8,128)(2,1)}, u32[]{:S(2)}, u32[]{:S(2)}) async-start(bf16[8,64,2048]{2,1,0:T(8,128)(2,1)} %bitcast.42), calls=%async_computation.1 | async-start | bytes 4194304 | tf_op jit(solution)/shard_map/chunk0/all_to_all | solution.py:45
  113.8 0.8 copy-start.1

commit v4 on v2

v4 whole, which is shorter than its diff:
```python
import jax
import jax.numpy as jnp
from jax import lax
from jax.sharding import PartitionSpec as P


def slot_matrices(routes, gate_values, groups, capacity):
    tok_rows = routes.shape[0]
    experts = jnp.arange(groups, dtype=jnp.int32)
    matched = routes[:, :, None] == experts[None, None, :]
    named = jnp.any(matched, axis=1)
    weight = jnp.sum(jnp.where(matched, gate_values.astype(jnp.float32)[:, :, None], 0.0), axis=1)
    position = jnp.cumsum(named.astype(jnp.int32), axis=0) - 1
    slots = jnp.arange(capacity, dtype=jnp.int32)
    hit = named[:, :, None] & (position[:, :, None] == slots[None, None, :])
    weighted = jnp.where(hit, weight[:, :, None], 0.0).astype(jnp.bfloat16)
    picks = hit.astype(jnp.bfloat16).reshape(tok_rows, groups * capacity).T
    return picks, weighted.reshape(tok_rows, groups * capacity)


def local(tokens, routes, gate_values, weight_in, weight_out):
    groups = lax.axis_size("expert")
    tok_rows, width = tokens.shape
    capacity = min(tok_rows, 2 * tok_rows * routes.shape[1] // groups)
    hidden_units = weight_out.shape[1]
    picks, weighted = lax.optimization_barrier(
        slot_matrices(routes, gate_values, groups, capacity)
    )
    outgoing = jnp.dot(picks, tokens, preferred_element_type=jnp.float32).astype(jnp.bfloat16)
    rows = lax.all_to_all(outgoing, "expert", 0, 0, tiled=True)
    projected = jnp.dot(rows, weight_in[0], preferred_element_type=jnp.float32)
    hidden = (jax.nn.silu(projected[:, :hidden_units]) * projected[:, hidden_units:]).astype(
        jnp.bfloat16
    )
    expert_out = jnp.dot(hidden, weight_out[0], preferred_element_type=jnp.float32)
    returned = lax.all_to_all(expert_out.astype(jnp.bfloat16), "expert", 0, 0, tiled=True)
    mixed = jnp.dot(weighted, returned, preferred_element_type=jnp.float32)
    return mixed.astype(jnp.bfloat16)


def solution(mesh):
    in_specs = (
        P(("dp", "expert"), None),
        P(("dp", "expert"), None),
        P(("dp", "expert"), None),
        P("expert", None, None),
        P("expert", None, None),
    )
    out_specs = P(("dp", "expert"), None)
    return jax.shard_map(local, mesh=mesh, in_specs=in_specs, out_specs=out_specs, check_vma=False)
```

time: 142 us -> 130 us (0.915); the launches traced: 142 us -> 128 us
  waiting for transfers between devices: 57.1 us -> 0 us
  blocking collectives: 56.7 us -> 109 us
  matrix products: 20.3 us -> 13.9 us
  starting transfers between devices: 6.29 us -> 0 us
  other arithmetic: 1.54 us -> 3.37 us
    all_to_all x1 -> x0, waiting for transfers between devices: 57.1 us -> none  [local(): returned = lax.all_to_all(expert_out, 'expert', 0, 0, tiled=True)]
    all_to_all x1 -> x2, blocking collectives: 56.7 us -> 109 us  [the longest x1 56.7 us: local(): rows = lax.all_to_all(outgoing, 'expert', 0, 0, tiled=True)]
    all_to_all x1 -> x0, starting transfers between devices: 6.29 us -> none  [local(): returned = lax.all_to_all(expert_out, 'expert', 0, 0, tiled=True)]
    dot_general x2, matrix products: 8.56 us -> 3.56 us  [the longest x1 2.27 us: local(): mixed = jnp.dot(weighted, returned, preferred_element_type=jnp.float32)]
  transfers between devices with their start and end apart: 1 -> 0, of which waited for: 1 -> 0; matrix products, arithmetic and copies ran while one was open for 0% -> 0% of each run, Pallas kernels for 0% -> 0%
where the time goes in v4:
time: 130 us; the launch traced here: 128 us
  blocking collectives  109 us (84%)
  matrix products  13.9 us (11%)
  other arithmetic  3.37 us (3%)
  local copies, waits for them, and re-layouts  1.65 us (1%)
    all_to_all x1, blocking collectives, local(): rows = lax.all_to_all(outgoing, 'expert', 0, 0, tiled=True)  56.7 us
    all_to_all x1, blocking collectives, local(): lax.all_to_all(expert_out.astype(jnp.bfloat16), 'expert', 0, 0, tiled=True)  52.3 us
    dot_general x1, matrix products, local(): projected = jnp.dot(rows, weight_in[0], preferred_element_type=jnp.float32)  6.65 us
    dot_general x1, matrix products, local(): jnp.dot(hidden, weight_out[0], preferred_element_type=jnp.float32)  3.71 us

profile of v4, /device:TPU:38, one launch (start us, length us, event | category | flops | bytes accessed | tf_op | source)
XLA Modules:
  0.0 128.1 jit_solution(12002444746742790868)
XLA Ops:
  0.0 0.8 fusion.8
  0.9 0.2 copy.12
  1.0 0.7 convert_element_type.27
  1.7 0.7 select_reduce_fusion
  2.4 0.6 reduce-window.6
  3.0 0.2 slice_reduce_fusion
  3.2 0.1 add_bitcast_fusion
  3.3 0.1 copy.14
  3.4 0.1 copy.13
  3.6 0.0 copy-start.1
  3.6 0.3 and.12
  3.9 0.3 broadcast_in_dim.35
  4.2 0.3 eq.37
  4.6 0.4 fusion.6
  5.0 0.1 convert_bitcast_fusion
  5.1 0.0 slice-start
  5.1 1.3 %convolution_convert_fusion = bf16[1024,2048]{1,0:T(8,128)(2,1)S(1)} fusion(bf16[1024,256]{0,1:T(8,128)(2,1)S(1)} %convert_bitcast_fusion, bf16[256,2048]{1,0:T(8,128)(2,1)S(1)} %copy-done.1), kind=kOutput, calls=%fused_computation.2 | convolution fusion | flops 1075838976 | bytes 5767168 | tf_op jit(solution)/shard_map/dot_general | solution.py:29
  6.4 0.0 slice-start.1
  6.4 56.7 %all_to_all.24 = bf16[8,128,2048]{2,1,0:T(8,128)(2,1)S(1)} all-to-all(bf16[8,128,2048]{2,1,0:T(8,128)(2,1)S(1)} %bitcast.42), channel_id=1, replica_groups=mesh['dp'=32,'expert'=8] {'expert'}, dimensions={0} | all-to-all | bytes 8388608 | tf_op jit(solution)/shard_map/all_to_all | solution.py:30
  63.1 0.0 slice-done.1
  63.1 6.7 %fusion = f32[1024,1536]{1,0:T(8,128)S(1)} fusion(bf16[1024,2048]{1,0:T(8,128)(2,1)S(1)} %bitcast.45, bf16[1,2048,1536]{2,1,0:T(8,128)(2,1)S(1)} %bitcast.50), kind=kOutput, calls=%fused_computation | convolution fusion | flops 6442450944 | bytes 16777216 | tf_op jit(solution)/shard_map/dot_general | solution.py:31
  69.8 3.7 %convolution_convert_fusion.1 = bf16[1024,2048]{1,0:T(8,128)(2,1)S(1)} fusion(bf16[1,768,2048]{2,1,0:T(8,128)(2,1)S(1)} %copy-done, f32[1024,1536]{1,0:T(8,128)S(1)} %fusion), kind=kOutput, calls=%fused_computation.3 | convolution fusion | flops 3228041216 | bytes 13631488 | tf_op jit(solution)/shard_map/dot_general | solution.py:35
  73.5 52.3 %all_to_all.25 = bf16[8,128,2048]{2,1,0:T(8,128)(2,1)S(1)} all-to-all(bf16[8,128,2048]{2,1,0:T(8,128)(2,1)S(1)} %bitcast.46), channel_id=1, replica_groups=mesh['dp'=32,'expert'=8] {'expert'}, dimensions={0} | all-to-all | bytes 8388608 | tf_op jit(solution)/shard_map/all_to_all | solution.py:36
  125.8 2.3 %convolution_convert_fusion.2 = bf16[256,2048]{1,0:T(8,128)(2,1)} fusion(bf16[256,1024]{1,0:T(8,128)(2,1)S(1)} %get-tuple-element.7, bf16[1024,2048]{1,0:T(8,128)(2,1)S(1)} %bitcast.44), kind=kOutput, calls=%fused_computation.7 | convolution fusion | flops 1074266112 | bytes 5767168 | tf_op jit(solution)/shard_map/dot_general | solution.py:37
  (9 shorter events, 0.1 us)
Async XLA Ops:
  0.0 69.8 %copy-start = (bf16[1,768,2048]{2,1,0:T(8,128)(2,1)S(1)}, bf16[1,768,2048]{2,1,0:T(8,128)(2,1)}, u32[]{:S(2)}) copy-start(bf16[1,768,2048]{2,1,0:T(8,128)(2,1)} %param.9) | copy-start | bytes 9437188
  3.6 1.5 %copy-start.1 = (bf16[256,2048]{1,0:T(8,128)(2,1)S(1)}, bf16[256,2048]{1,0:T(8,128)(2,1)}, u32[]{:S(2)}) copy-start(bf16[256,2048]{1,0:T(8,128)(2,1)} %param.5) | copy-start | bytes 3145732
  5.1 58.1 %slice-start = ((s8[6291456]{0:T(1024)(128)(4,1)}), s8[4194304]{0:T(1024)(128)(4,1)S(1)}, s32[]{:S(2)}) async-start(s8[6291456]{0:T(1024)(128)(4,1)} %bitcast.49), calls=%async_computation.2 | async-start | bytes 8388608
  6.4 56.8 %slice-start.1 = ((s8[6291456]{0:T(1024)(128)(4,1)}), s8[2097152]{0:T(1024)(128)(4,1)S(1)}, s32[]{:S(2)}) async-start(s8[6291456]{0:T(1024)(128)(4,1)} %bitcast.49), calls=%async_computation.3 | async-start | bytes 4194304

commit v5 on v4

--- a/solution.py
+++ b/solution.py
@@ -10,12 +10,14 @@
     matched = routes[:, :, None] == experts[None, None, :]
     named = jnp.any(matched, axis=1)
     weight = jnp.sum(jnp.where(matched, gate_values.astype(jnp.float32)[:, :, None], 0.0), axis=1)
-    position = jnp.cumsum(named.astype(jnp.int32), axis=0) - 1
-    slots = jnp.arange(capacity, dtype=jnp.int32)
-    hit = named[:, :, None] & (position[:, :, None] == slots[None, None, :])
+    order = jnp.arange(tok_rows, dtype=jnp.int32)
+    earlier = (order[:, None] >= order[None, :]).astype(jnp.bfloat16)
+    count = jnp.dot(earlier, named.astype(jnp.bfloat16), preferred_element_type=jnp.float32)
+    slots = jnp.arange(capacity, dtype=jnp.float32) + 1.0
+    hit = named[:, :, None] & (count[:, :, None] == slots[None, None, :])
     weighted = jnp.where(hit, weight[:, :, None], 0.0).astype(jnp.bfloat16)
-    picks = hit.astype(jnp.bfloat16).reshape(tok_rows, groups * capacity).T
-    return picks, weighted.reshape(tok_rows, groups * capacity)
+    picks = hit.astype(jnp.bfloat16)
+    return (picks.reshape(tok_rows, groups * capacity), weighted.reshape(tok_rows, groups * capacity))
 
 
 def local(tokens, routes, gate_values, weight_in, weight_out):
@@ -26,7 +28,9 @@
     picks, weighted = lax.optimization_barrier(
         slot_matrices(routes, gate_values, groups, capacity)
     )
-    outgoing = jnp.dot(picks, tokens, preferred_element_type=jnp.float32).astype(jnp.bfloat16)
+    outgoing = lax.dot_general(
+        picks, tokens, (((0,), (0,)), ((), ())), preferred_element_type=jnp.float32
+    ).astype(jnp.bfloat16)
     rows = lax.all_to_all(outgoing, "expert", 0, 0, tiled=True)
     projected = jnp.dot(rows, weight_in[0], preferred_element_type=jnp.float32)
     hidden = (jax.nn.silu(projected[:, :hidden_units]) * projected[:, hidden_units:]).astype(

time: 130 us -> 129 us (level)
  no operation moved by 1% of the time
where the time goes in v5:
time: 129 us; the launch traced here: 127 us
  blocking collectives  109 us (84%)
  matrix products  14.1 us (11%)
  other arithmetic  2.7 us (2%)
  local copies, waits for them, and re-layouts  1.31 us (1%)
    all_to_all x1, blocking collectives, local(): rows = lax.all_to_all(outgoing, 'expert', 0, 0, tiled=True)  56.7 us
    all_to_all x1, blocking collectives, local(): lax.all_to_all(expert_out.astype(jnp.bfloat16), 'expert', 0, 0, tiled=True)  52.3 us
    dot_general x1, matrix products, local(): projected = jnp.dot(rows, weight_in[0], preferred_element_type=jnp.float32)  6.65 us
    dot_general x1, matrix products, local(): jnp.dot(hidden, weight_out[0], preferred_element_type=jnp.float32)  3.7 us

profile of v5, /device:TPU:38, one launch (start us, length us, event | category | flops | bytes accessed | tf_op | source)
XLA Modules:
  0.0 127.2 jit_solution(15170202248251416455)
XLA Ops:
  0.0 0.0 copy-start
  0.0 0.8 fusion.9
  0.9 0.2 copy.9
  1.0 0.2 fusion.8
  1.2 0.7 convert_element_type.26
  1.9 0.7 select_reduce_fusion
  2.6 0.1 copy.11
  2.7 0.3 and.12
  3.0 0.3 broadcast_in_dim.37
  3.4 0.3 eq.37
  3.7 0.4 fusion.6
  4.1 0.1 convert_element_type.25
  4.2 0.0 copy-done.1
  4.2 0.0 slice-start
  4.2 1.3 %convolution_convert_fusion = bf16[1024,2048]{1,0:T(8,128)(2,1)S(1)} fusion(bf16[256,1024]{1,0:T(8,128)(2,1)S(1)} %convert_element_type.25, bf16[256,2048]{1,0:T(8,128)(2,1)S(1)} %copy-done.1), kind=kOutput, calls=%fused_computation.2 | convolution fusion | flops 1075838976 | bytes 5767168 | tf_op jit(solution)/shard_map/dot_general | solution.py:31
  5.5 0.0 slice-start.1
  5.5 56.7 %all_to_all.24 = bf16[8,128,2048]{2,1,0:T(8,128)(2,1)S(1)} all-to-all(bf16[8,128,2048]{2,1,0:T(8,128)(2,1)S(1)} %bitcast.33), channel_id=1, replica_groups=mesh['dp'=32,'expert'=8] {'expert'}, dimensions={0} | all-to-all | bytes 8388608 | tf_op jit(solution)/shard_map/all_to_all | solution.py:34
  62.3 0.0 slice-done
  62.3 0.0 slice-done.1
  62.3 6.7 %fusion = f32[1024,1536]{1,0:T(8,128)S(1)} fusion(bf16[1024,2048]{1,0:T(8,128)(2,1)S(1)} %bitcast.36, bf16[1,2048,1536]{2,1,0:T(8,128)(2,1)S(1)} %bitcast.41), kind=kOutput, calls=%fused_computation | convolution fusion | flops 6442450944 | bytes 16777216 | tf_op jit(solution)/shard_map/dot_general | solution.py:35
  68.9 0.0 copy-done
  68.9 3.7 %convolution_convert_fusion.1 = bf16[1024,2048]{1,0:T(8,128)(2,1)S(1)} fusion(bf16[1,768,2048]{2,1,0:T(8,128)(2,1)S(1)} %copy-done, f32[1024,1536]{1,0:T(8,128)S(1)} %fusion), kind=kOutput, calls=%fused_computation.3 | convolution fusion | flops 3228041216 | bytes 13631488 | tf_op jit(solution)/shard_map/dot_general | solution.py:39
  72.7 52.3 %all_to_all.25 = bf16[8,128,2048]{2,1,0:T(8,128)(2,1)S(1)} all-to-all(bf16[8,128,2048]{2,1,0:T(8,128)(2,1)S(1)} %bitcast.37), channel_id=1, replica_groups=mesh['dp'=32,'expert'=8] {'expert'}, dimensions={0} | all-to-all | bytes 8388608 | tf_op jit(solution)/shard_map/all_to_all | solution.py:40
  125.0 2.3 %convolution_convert_fusion.2 = bf16[256,2048]{1,0:T(8,128)(2,1)} fusion(bf16[256,1024]{1,0:T(8,128)(2,1)S(1)} %get-tuple-element.7, bf16[1024,2048]{1,0:T(8,128)(2,1)S(1)} %bitcast.35), kind=kOutput, calls=%fused_computation.7 | convolution fusion | flops 1074266112 | bytes 5767168 | tf_op jit(solution)/shard_map/dot_general | solution.py:41
  (4 shorter events, 0.0 us)
Async XLA Ops:
  0.0 68.9 %copy-start = (bf16[1,768,2048]{2,1,0:T(8,128)(2,1)S(1)}, bf16[1,768,2048]{2,1,0:T(8,128)(2,1)}, u32[]{:S(2)}) copy-start(bf16[1,768,2048]{2,1,0:T(8,128)(2,1)} %param.9) | copy-start | bytes 9437188
  2.7 1.5 %copy-start.1 = (bf16[256,2048]{1,0:T(8,128)(2,1)S(1)}, bf16[256,2048]{1,0:T(8,128)(2,1)}, u32[]{:S(2)}) copy-start(bf16[256,2048]{1,0:T(8,128)(2,1)} %param.5) | copy-start | bytes 3145732
  4.2 58.1 %slice-start = ((s8[6291456]{0:T(1024)(128)(4,1)}), s8[4194304]{0:T(1024)(128)(4,1)S(1)}, s32[]{:S(2)}) async-start(s8[6291456]{0:T(1024)(128)(4,1)} %bitcast.40), calls=%async_computation.2 | async-start | bytes 8388608
  5.5 56.8 %slice-start.1 = ((s8[6291456]{0:T(1024)(128)(4,1)}), s8[2097152]{0:T(1024)(128)(4,1)S(1)}, s32[]{:S(2)}) async-start(s8[6291456]{0:T(1024)(128)(4,1)} %bitcast.40), calls=%async_computation.3 | async-start | bytes 4194304

commit v6 on v5

--- a/solution.py
+++ b/solution.py
@@ -6,18 +6,19 @@
 
 def slot_matrices(routes, gate_values, groups, capacity):
     tok_rows = routes.shape[0]
-    experts = jnp.arange(groups, dtype=jnp.int32)
-    matched = routes[:, :, None] == experts[None, None, :]
-    named = jnp.any(matched, axis=1)
-    weight = jnp.sum(jnp.where(matched, gate_values.astype(jnp.float32)[:, :, None], 0.0), axis=1)
+    column = jnp.arange(groups * capacity, dtype=jnp.int32)[None, :]
+    expert_of, slot_of = column // capacity, column % capacity
+    first = routes[:, 0:1] == expert_of
+    second = routes[:, 1:2] == expert_of
+    named = first | second
     order = jnp.arange(tok_rows, dtype=jnp.int32)
     earlier = (order[:, None] >= order[None, :]).astype(jnp.bfloat16)
     count = jnp.dot(earlier, named.astype(jnp.bfloat16), preferred_element_type=jnp.float32)
-    slots = jnp.arange(capacity, dtype=jnp.float32) + 1.0
-    hit = named[:, :, None] & (count[:, :, None] == slots[None, None, :])
-    weighted = jnp.where(hit, weight[:, :, None], 0.0).astype(jnp.bfloat16)
-    picks = hit.astype(jnp.bfloat16)
-    return (picks.reshape(tok_rows, groups * capacity), weighted.reshape(tok_rows, groups * capacity))
+    hit = named & (count == (slot_of + 1).astype(jnp.float32))
+    gates = gate_values.astype(jnp.float32)
+    weight = jnp.where(first, gates[:, 0:1], jnp.where(second, gates[:, 1:2], 0.0))
+    weighted = jnp.where(hit, weight, 0.0).astype(jnp.bfloat16)
+    return hit.astype(jnp.bfloat16), weighted
 
 
 def local(tokens, routes, gate_values, weight_in, weight_out):

time: 129 us -> 127 us (0.984)
  other arithmetic: 2.7 us -> 0.33 us
    slice x0 -> x2, local copies, waits for them, and re-layouts: none -> 1.67 us  [the longest x1 0.86 us: slot_matrices(): first = routes[:, 0:1] == expert_of]
where the time goes in v6:
time: 127 us; the launch traced here: 126 us
  blocking collectives  109 us (86%)
  matrix products  14.5 us (11%)
  local copies, waits for them, and re-layouts  1.69 us (1%)
    all_to_all x1, blocking collectives, local(): rows = lax.all_to_all(outgoing, 'expert', 0, 0, tiled=True)  56.7 us
    all_to_all x1, blocking collectives, local(): lax.all_to_all(expert_out.astype(jnp.bfloat16), 'expert', 0, 0, tiled=True)  52.3 us
    dot_general x1, matrix products, local(): projected = jnp.dot(rows, weight_in[0], preferred_element_type=jnp.float32)  6.65 us
    dot_general x1, matrix products, local(): jnp.dot(hidden, weight_out[0], preferred_element_type=jnp.float32)  3.7 us

profile of v6, /device:TPU:38, one launch (start us, length us, event | category | flops | bytes accessed | tf_op | source)
XLA Modules:
  0.0 125.7 jit_solution(17657211568756817533)
XLA Ops:
  0.0 0.0 copy-start
  0.0 0.0 copy-start.1
  0.0 0.9 fusion.22
  0.9 0.8 fusion.23
  1.7 0.6 fusion.24
  2.3 0.3 fusion.8
  2.6 0.0 copy-done.1
  2.7 0.0 slice-start
  2.7 1.3 %convolution_convert_fusion = bf16[1024,2048]{1,0:T(8,128)(2,1)S(1)} fusion(bf16[256,1024]{1,0:T(8,128)(2,1)S(1)} %get-tuple-element.8, bf16[256,2048]{1,0:T(8,128)(2,1)S(1)} %copy-done.1), kind=kOutput, calls=%fused_computation.2 | convolution fusion | flops 1075838976 | bytes 5767168 | tf_op jit(solution)/shard_map/dot_general | solution.py:32
  4.0 0.0 slice-start.1
  4.0 56.7 %all_to_all.24 = bf16[8,128,2048]{2,1,0:T(8,128)(2,1)S(1)} all-to-all(bf16[8,128,2048]{2,1,0:T(8,128)(2,1)S(1)} %bitcast.19), channel_id=1, replica_groups=mesh['dp'=32,'expert'=8] {'expert'}, dimensions={0} | all-to-all | bytes 8388608 | tf_op jit(solution)/shard_map/all_to_all | solution.py:35
  60.7 0.0 slice-done
  60.7 0.0 slice-done.1
  60.7 6.6 %fusion = f32[1024,1536]{1,0:T(8,128)S(1)} fusion(bf16[1024,2048]{1,0:T(8,128)(2,1)S(1)} %bitcast.21, bf16[1,2048,1536]{2,1,0:T(8,128)(2,1)S(1)} %bitcast.30), kind=kOutput, calls=%fused_computation | convolution fusion | flops 6442450944 | bytes 16777216 | tf_op jit(solution)/shard_map/dot_general | solution.py:36
  67.4 0.0 copy-done
  67.4 3.7 %convolution_convert_fusion.1 = bf16[1024,2048]{1,0:T(8,128)(2,1)S(1)} fusion(bf16[1,768,2048]{2,1,0:T(8,128)(2,1)S(1)} %copy-done, f32[1024,1536]{1,0:T(8,128)S(1)} %fusion), kind=kOutput, calls=%fused_computation.3 | convolution fusion | flops 3228041216 | bytes 13631488 | tf_op jit(solution)/shard_map/dot_general | solution.py:40
  71.1 52.3 %all_to_all.25 = bf16[8,128,2048]{2,1,0:T(8,128)(2,1)S(1)} all-to-all(bf16[8,128,2048]{2,1,0:T(8,128)(2,1)S(1)} %bitcast.22), channel_id=1, replica_groups=mesh['dp'=32,'expert'=8] {'expert'}, dimensions={0} | all-to-all | bytes 8388608 | tf_op jit(solution)/shard_map/all_to_all | solution.py:41
  123.4 2.3 %convolution_convert_fusion.2 = bf16[256,2048]{1,0:T(8,128)(2,1)} fusion(bf16[256,1024]{1,0:T(8,128)(2,1)S(1)} %fusion.8, bf16[1024,2048]{1,0:T(8,128)(2,1)S(1)} %bitcast.20), kind=kOutput, calls=%fused_computation.7 | convolution fusion | flops 1074266112 | bytes 5767168 | tf_op jit(solution)/shard_map/dot_general | solution.py:42
  (2 shorter events, 0.0 us)
Async XLA Ops:
  0.0 67.4 %copy-start = (bf16[1,768,2048]{2,1,0:T(8,128)(2,1)S(1)}, bf16[1,768,2048]{2,1,0:T(8,128)(2,1)}, u32[]{:S(2)}) copy-start(bf16[1,768,2048]{2,1,0:T(8,128)(2,1)} %param.9) | copy-start | bytes 9437188
  0.0 2.6 %copy-start.1 = (bf16[256,2048]{1,0:T(8,128)(2,1)S(1)}, bf16[256,2048]{1,0:T(8,128)(2,1)}, u32[]{:S(2)}) copy-start(bf16[256,2048]{1,0:T(8,128)(2,1)} %param.5) | copy-start | bytes 3145732
  2.7 58.1 %slice-start = ((s8[6291456]{0:T(1024)(128)(4,1)}), s8[4194304]{0:T(1024)(128)(4,1)S(1)}, s32[]{:S(2)}) async-start(s8[6291456]{0:T(1024)(128)(4,1)} %bitcast.29), calls=%async_computation.2 | async-start | bytes 8388608
  4.0 56.7 %slice-start.1 = ((s8[6291456]{0:T(1024)(128)(4,1)}), s8[2097152]{0:T(1024)(128)(4,1)S(1)}, s32[]{:S(2)}) async-start(s8[6291456]{0:T(1024)(128)(4,1)} %bitcast.29), calls=%async_computation.3 | async-start | bytes 4194304

commit v7 on v6

--- a/solution.py
+++ b/solution.py
@@ -37,10 +37,15 @@
     hidden = (jax.nn.silu(projected[:, :hidden_units]) * projected[:, hidden_units:]).astype(
         jnp.bfloat16
     )
-    expert_out = jnp.dot(hidden, weight_out[0], preferred_element_type=jnp.float32)
-    returned = lax.all_to_all(expert_out.astype(jnp.bfloat16), "expert", 0, 0, tiled=True)
-    mixed = jnp.dot(weighted, returned, preferred_element_type=jnp.float32)
-    return mixed.astype(jnp.bfloat16)
+    half = width // 2
+    parts = []
+    for k in range(2):
+        with jax.named_scope(f"cols{k}"):
+            cols = slice(k * half, (k + 1) * half)
+            expert_out = jnp.dot(hidden, weight_out[0][:, cols], preferred_element_type=jnp.float32)
+            returned = lax.all_to_all(expert_out.astype(jnp.bfloat16), "expert", 0, 0, tiled=True)
+            parts.append(jnp.dot(weighted, returned, preferred_element_type=jnp.float32).astype(jnp.bfloat16))
+    return jnp.concatenate(parts, axis=1)
 
 
 def solution(mesh):

time: 127 us -> 143 us (1.13)
  blocking collectives: 109 us -> 56.7 us
  waiting for transfers between devices: 0 us -> 45.7 us
  starting transfers between devices: 0 us -> 12.2 us
  matrix products: 14.5 us -> 21.7 us
  other arithmetic: 0.33 us -> 3.14 us
    all_to_all x1 -> x0, blocking collectives: 52.3 us -> none  [local(): lax.all_to_all(expert_out.astype(jnp.bfloat16), 'expert', 0, 0, tiled=True)]
    all_to_all x0 -> x2, waiting for transfers between devices: none -> 45.7 us  [local(): lax.all_to_all(expert_out.astype(jnp.bfloat16), 'expert', 0, 0, tiled=True)]
    all_to_all x0 -> x2, starting transfers between devices: none -> 12.2 us  [local(): lax.all_to_all(expert_out.astype(jnp.bfloat16), 'expert', 0, 0, tiled=True)]
    dot_general x2 -> x4, matrix products: 5.97 us -> 13.1 us  [the longest x2 8.12 us: local(): jnp.dot(hidden, weight_out[0][:, cols], preferred_element_type=jnp.float32)]
  transfers between devices with their start and end apart: 0 -> 2, of which waited for: 0 -> 2; matrix products, arithmetic and copies ran while one was open for 0% -> 5% of each run, Pallas kernels for 0% -> 0%
where the time goes in v7:
time: 143 us; the launch traced here: 142 us
  blocking collectives  56.7 us (40%)
  waiting for transfers between devices  45.7 us (32%)
  matrix products  21.7 us (15%)
  starting transfers between devices  12.2 us (9%)
  other arithmetic  3.14 us (2%)
  local copies, waits for them, and re-layouts  2.48 us (2%)
    all_to_all x1, blocking collectives, local(): rows = lax.all_to_all(outgoing, 'expert', 0, 0, tiled=True)  56.7 us
    all_to_all x2, waiting for transfers between devices, local(): lax.all_to_all(expert_out.astype(jnp.bfloat16), 'expert', 0, 0, tiled=True)  45.7 us
    all_to_all x2, starting transfers between devices, local(): lax.all_to_all(expert_out.astype(jnp.bfloat16), 'expert', 0, 0, tiled=True)  12.2 us
    dot_general x2, matrix products, local(): jnp.dot(hidden, weight_out[0][:, cols], preferred_element_type=jnp.float32)  8.12 us
    dot_general x1, matrix products, local(): projected = jnp.dot(rows, weight_in[0], preferred_element_type=jnp.float32)  6.65 us
    dot_general x2, matrix products, local(): jnp.dot(weighted, returned, preferred_element_type=jnp.float32)  5.02 us
  transfers between devices with their start and end apart: 2, of which 2 were waited for; matrix products, arithmetic and copies ran while one was open for 5% of the time, Pallas kernels for 0%

profile of v7, /device:TPU:38, one launch (start us, length us, event | category | flops | bytes accessed | tf_op | source)
XLA Modules:
  0.0 142.0 jit_solution(16108273744990078075)
XLA Ops:
  0.0 0.0 copy-start
  0.0 0.8 fusion.20
  0.8 0.8 fusion.21
  1.6 0.6 fusion.22
  2.2 1.1 fusion.7
  3.3 0.0 copy-done
  3.3 1.3 convolution_convert_fusion
  4.6 0.0 slice-start.1
  4.6 56.7 %all_to_all.36 = bf16[8,128,2048]{2,1,0:T(8,128)(2,1)S(1)} all-to-all(bf16[8,128,2048]{2,1,0:T(8,128)(2,1)S(1)} %bitcast.23), channel_id=1, replica_groups=mesh['dp'=32,'expert'=8] {'expert'}, dimensions={0} | all-to-all | bytes 8388608 | tf_op jit(solution)/shard_map/all_to_all | solution.py:35
  61.4 0.0 slice-done.1
  61.4 6.7 %fusion = f32[1024,1536]{1,0:T(8,128)S(1)} fusion(bf16[1024,2048]{1,0:T(8,128)(2,1)S(1)} %bitcast.24, bf16[1,2048,1536]{2,1,0:T(8,128)(2,1)S(1)} %bitcast.35), kind=kOutput, calls=%fused_computation | convolution fusion | flops 6442450944 | bytes 16777216 | tf_op jit(solution)/shard_map/dot_general | solution.py:36
  68.0 0.0 copy-start.3
  68.0 1.0 fusion.2
  69.0 0.9 copy-done.3
  69.9 3.1 %convolution_convert_fusion.1 = bf16[1024,1024]{1,0:T(8,128)(2,1)} fusion(bf16[1024,768]{1,0:T(8,128)(2,1)S(1)} %fusion.2, bf16[768,2048]{1,0:T(8,128)(2,1)S(1)} %bitcast.37), kind=kOutput, calls=%fused_computation.5 | convolution fusion | flops 1611661312 | bytes 5242880 | tf_op jit(solution)/shard_map/cols1/dot_general | solution.py:45
  73.0 5.2 %all-to-all-start.2 = ((bf16[8,128,1024]{2,1,0:T(8,128)(2,1)}), bf16[8,128,1024]{2,1,0:T(8,128)(2,1)S(1)}, u32[]{:S(2)}, u32[]{:S(2)}) async-start(bf16[8,128,1024]{2,1,0:T(8,128)(2,1)} %bitcast.27), calls=%async_computation.2 | async-start | bytes 4194304 | tf_op jit(solution)/shard_map/cols1/all_to_all | solution.py:46
  78.3 5.0 %convolution_convert_fusion.2 = bf16[1024,1024]{1,0:T(8,128)(2,1)} fusion(bf16[1024,768]{1,0:T(8,128)(2,1)} %copy-done.1, bf16[768,2048]{1,0:T(8,128)(2,1)} %bitcast.36), kind=kOutput, calls=%fused_computation.6 | convolution fusion | flops 1611661312 | bytes 5242880 | tf_op jit(solution)/shard_map/cols0/dot_general | solution.py:45
  83.3 19.7 %all-to-all-done.2 = bf16[8,128,1024]{2,1,0:T(8,128)(2,1)S(1)} async-done(((bf16[8,128,1024]{2,1,0:T(8,128)(2,1)}), bf16[8,128,1024]{2,1,0:T(8,128)(2,1)S(1)}, u32[]{:S(2)}, u32[]{:S(2)}) %all-to-all-start.2) | async-done | bytes 2097184 | tf_op jit(solution)/shard_map/cols1/all_to_all | solution.py:46
  103.0 6.9 %all-to-all-start.1 = ((bf16[8,128,1024]{2,1,0:T(8,128)(2,1)}), bf16[8,128,1024]{2,1,0:T(8,128)(2,1)}, u32[]{:S(2)}, u32[]{:S(2)}) async-start(bf16[8,128,1024]{2,1,0:T(8,128)(2,1)} %bitcast.26), calls=%async_computation.1 | async-start | bytes 4194304 | tf_op jit(solution)/shard_map/cols0/all_to_all | solution.py:46
  109.9 2.5 %convolution_convert_fusion.3 = bf16[256,1024]{1,0:T(8,128)(2,1)} fusion(bf16[256,1024]{1,0:T(8,128)(2,1)} %fusion.7, bf16[1024,1024]{1,0:T(8,128)(2,1)S(1)} %bitcast.25), kind=kOutput, calls=%fused_computation.12 | convolution fusion | flops 537133056 | bytes 3145728 | tf_op jit(solution)/shard_map/cols1/dot_general | solution.py:47
  112.5 26.0 %all-to-all-done.1 = bf16[8,128,1024]{2,1,0:T(8,128)(2,1)} async-done(((bf16[8,128,1024]{2,1,0:T(8,128)(2,1)}), bf16[8,128,1024]{2,1,0:T(8,128)(2,1)}, u32[]{:S(2)}, u32[]{:S(2)}) %all-to-all-start.1) | async-done | bytes 2097184 | tf_op jit(solution)/shard_map/cols0/all_to_all | solution.py:46
  138.5 2.5 %convolution_convert_fusion.4 = bf16[256,1024]{1,0:T(8,128)(2,1)S(1)} fusion(bf16[256,1024]{1,0:T(8,128)(2,1)} %fusion.7, bf16[1024,1024]{1,0:T(8,128)(2,1)} %bitcast.9), kind=kOutput, calls=%fused_computation.13 | convolution fusion | flops 537133056 | bytes 3145728 | tf_op jit(solution)/shard_map/cols0/dot_general | solution.py:47
  141.0 0.0 copy-done.2
  141.0 1.1 pad_maximum_fusion
  (7 shorter events, 0.0 us)
Async XLA Ops:
  0.0 3.3 %copy-start = (bf16[256,2048]{1,0:T(8,128)(2,1)S(1)}, bf16[256,2048]{1,0:T(8,128)(2,1)}, u32[]{:S(2)}) copy-start(bf16[256,2048]{1,0:T(8,128)(2,1)} %param.5) | copy-start | bytes 3145732
  3.3 58.1 %slice-start = ((s8[6291456]{0:T(1024)(128)(4,1)}), s8[4194304]{0:T(1024)(128)(4,1)S(1)}, s32[]{:S(2)}) async-start(s8[6291456]{0:T(1024)(128)(4,1)} %bitcast.34), calls=%async_computation.3 | async-start | bytes 8388608
  4.6 56.8 %slice-start.1 = ((s8[6291456]{0:T(1024)(128)(4,1)}), s8[2097152]{0:T(1024)(128)(4,1)S(1)}, s32[]{:S(2)}) async-start(s8[6291456]{0:T(1024)(128)(4,1)} %bitcast.34), calls=%async_computation.4 | async-start | bytes 4194304
  68.0 1.9 %copy-start.3 = (bf16[1,768,2048]{2,1,0:T(8,128)(2,1)S(1)}, bf16[1,768,2048]{2,1,0:T(8,128)(2,1)}, u32[]{:S(2)}) copy-start(bf16[1,768,2048]{2,1,0:T(8,128)(2,1)} %param.9) | copy-start | bytes 9437188
  69.0 4.0 %copy-start.1 = (bf16[1024,768]{1,0:T(8,128)(2,1)}, bf16[1024,768]{1,0:T(8,128)(2,1)S(1)}, u32[]{:S(2)}) copy-start(bf16[1024,768]{1,0:T(8,128)(2,1)S(1)} %fusion.2) | copy-start | bytes 4718596
  73.0 30.0 %all-to-all-start.2 = ((bf16[8,128,1024]{2,1,0:T(8,128)(2,1)}), bf16[8,128,1024]{2,1,0:T(8,128)(2,1)S(1)}, u32[]{:S(2)}, u32[]{:S(2)}) async-start(bf16[8,128,1024]{2,1,0:T(8,128)(2,1)} %bitcast.27), calls=%async_computation.2 | async-start | bytes 4194304 | tf_op jit(solution)/shard_map/cols1/all_to_all | solution.py:46
  103.0 35.5 %all-to-all-start.1 = ((bf16[8,128,1024]{2,1,0:T(8,128)(2,1)}), bf16[8,128,1024]{2,1,0:T(8,128)(2,1)}, u32[]{:S(2)}, u32[]{:S(2)}) async-start(bf16[8,128,1024]{2,1,0:T(8,128)(2,1)} %bitcast.26), calls=%async_computation.1 | async-start | bytes 4194304 | tf_op jit(solution)/shard_map/cols0/all_to_all | solution.py:46
  112.5 28.5 %copy-start.2 = (bf16[256,1024]{1,0:T(8,128)(2,1)S(1)}, bf16[256,1024]{1,0:T(8,128)(2,1)}, u32[]{:S(2)}) copy-start(bf16[256,1024]{1,0:T(8,128)(2,1)} %convolution_convert_fusion.3) | copy-start | bytes 1572868

commit v8 on v6

--- a/solution.py
+++ b/solution.py
@@ -33,10 +33,9 @@
         picks, tokens, (((0,), (0,)), ((), ())), preferred_element_type=jnp.float32
     ).astype(jnp.bfloat16)
     rows = lax.all_to_all(outgoing, "expert", 0, 0, tiled=True)
-    projected = jnp.dot(rows, weight_in[0], preferred_element_type=jnp.float32)
-    hidden = (jax.nn.silu(projected[:, :hidden_units]) * projected[:, hidden_units:]).astype(
-        jnp.bfloat16
-    )
+    gate_part = jnp.dot(rows, weight_in[0][:, :hidden_units], preferred_element_type=jnp.float32)
+    up_part = jnp.dot(rows, weight_in[0][:, hidden_units:], preferred_element_type=jnp.float32)
+    hidden = (jax.nn.silu(gate_part) * up_part).astype(jnp.bfloat16)
     expert_out = jnp.dot(hidden, weight_out[0], preferred_element_type=jnp.float32)
     returned = lax.all_to_all(expert_out.astype(jnp.bfloat16), "expert", 0, 0, tiled=True)
     mixed = jnp.dot(weighted, returned, preferred_element_type=jnp.float32)

time: 127 us -> 138 us (1.087)
  matrix products: 14.5 us -> 21.6 us
  local copies, waits for them, and re-layouts: 1.69 us -> 3.65 us
    dot_general x1, matrix products: 3.7 us -> 12.3 us  [local(): jnp.dot(hidden, weight_out[0], preferred_element_type=jnp.float32)]
    unnamed x8 -> x12, local copies, waits for them, and re-layouts: 0.02 us -> 1.98 us
    dot_general x1, matrix products: 6.65 us -> 5.14 us  [local(): jnp.dot(rows, weight_in[0][:, hidden_units:], preferred_element_type=jnp....]
where the time goes in v8:
time: 138 us; the launch traced here: 136 us
  blocking collectives  110 us (80%)
  matrix products  21.6 us (16%)
  local copies, waits for them, and re-layouts  3.65 us (3%)
    all_to_all x1, blocking collectives, local(): rows = lax.all_to_all(outgoing, 'expert', 0, 0, tiled=True)  56.7 us
    all_to_all x1, blocking collectives, local(): lax.all_to_all(expert_out.astype(jnp.bfloat16), 'expert', 0, 0, tiled=True)  53.2 us
    dot_general x1, matrix products, local(): jnp.dot(hidden, weight_out[0], preferred_element_type=jnp.float32)  12.3 us
    dot_general x1, matrix products, local(): jnp.dot(rows, weight_in[0][:, hidden_units:], preferred_element_type=jnp....  5.14 us

profile of v8, /device:TPU:38, one launch (start us, length us, event | category | flops | bytes accessed | tf_op | source)
XLA Modules:
  0.0 136.3 jit_solution(15590563020046639965)
XLA Ops:
  0.0 0.0 copy-start
  0.0 0.0 copy-start.2
  0.0 0.9 fusion.25
  0.9 0.8 fusion.26
  1.7 0.6 fusion.27
  2.3 1.1 fusion.9
  3.4 0.0 copy-done.2
  3.4 0.0 slice-start
  3.4 1.3 convolution_convert_fusion
  4.7 0.0 slice-start.1
  4.7 56.7 %all_to_all.24 = bf16[8,128,2048]{2,1,0:T(8,128)(2,1)S(1)} all-to-all(bf16[8,128,2048]{2,1,0:T(8,128)(2,1)S(1)} %bitcast.18), channel_id=1, replica_groups=mesh['dp'=32,'expert'=8] {'expert'}, dimensions={0} | all-to-all | bytes 8388608 | tf_op jit(solution)/shard_map/all_to_all | solution.py:35
  61.5 0.0 copy-start.1
  61.5 2.0 %copy-done.1 = bf16[8,128,2048]{2,1,0:T(8,128)(2,1)} copy-done((bf16[8,128,2048]{2,1,0:T(8,128)(2,1)}, bf16[8,128,2048]{2,1,0:T(8,128)(2,1)S(1)}, u32[]{:S(2)}) %copy-start.1) | copy-done | bytes 4194328
  63.4 0.0 slice-done
  63.4 0.0 slice-done.1
  63.4 5.1 %fusion = f32[1024,768]{1,0:T(8,128)} fusion(bf16[1024,2048]{1,0:T(8,128)(2,1)S(1)} %bitcast.19, bf16[2048,1536]{1,0:T(8,128)(2,1)S(1)} %bitcast.32), kind=kOutput, calls=%fused_computation.2 | convolution fusion | flops 3221225472 | bytes 10485760 | tf_op jit(solution)/shard_map/dot_general | solution.py:37
  68.6 0.0 copy-done
  68.6 12.3 %convolution_convert_fusion.1 = bf16[1024,2048]{1,0:T(8,128)(2,1)} fusion(bf16[1,768,2048]{2,1,0:T(8,128)(2,1)S(1)} %copy-done, f32[1024,768]{1,0:T(8,128)} %fusion, bf16[1024,2048]{1,0:T(8,128)(2,1)} %bitcast.20, bf16[2048,1536]{1,0:T(8,128)(2,1)} %bitcast.29), kind=kOutput, calls=%fused_computation.1 | convolution fusion | flops 6449266688 | bytes 17825792 | tf_op jit(solution)/shard_map/dot_general | solution.py:39
  80.9 0.0 copy-start.3
  80.9 53.2 %all_to_all.25 = bf16[8,128,2048]{2,1,0:T(8,128)(2,1)S(1)} all-to-all(bf16[8,128,2048]{2,1,0:T(8,128)(2,1)} %bitcast.21), channel_id=1, replica_groups=mesh['dp'=32,'expert'=8] {'expert'}, dimensions={0} | all-to-all | bytes 8388608 | tf_op jit(solution)/shard_map/all_to_all | solution.py:40
  134.1 0.0 copy-done.3
  134.1 2.2 %convolution_convert_fusion.2 = bf16[256,2048]{1,0:T(8,128)(2,1)} fusion(bf16[256,1024]{1,0:T(8,128)(2,1)S(1)} %copy-done.3, bf16[1024,2048]{1,0:T(8,128)(2,1)S(1)} %bitcast.22), kind=kOutput, calls=%fused_computation.8 | convolution fusion | flops 1074266112 | bytes 5767168 | tf_op jit(solution)/shard_map/dot_general | solution.py:41
  (2 shorter events, 0.0 us)
Async XLA Ops:
  0.0 68.6 %copy-start = (bf16[1,768,2048]{2,1,0:T(8,128)(2,1)S(1)}, bf16[1,768,2048]{2,1,0:T(8,128)(2,1)}, u32[]{:S(2)}) copy-start(bf16[1,768,2048]{2,1,0:T(8,128)(2,1)} %param.9) | copy-start | bytes 9437188
  0.0 3.4 %copy-start.2 = (bf16[256,2048]{1,0:T(8,128)(2,1)S(1)}, bf16[256,2048]{1,0:T(8,128)(2,1)}, u32[]{:S(2)}) copy-start(bf16[256,2048]{1,0:T(8,128)(2,1)} %param.5) | copy-start | bytes 3145732
  3.4 60.0 %slice-start = ((s8[6291456]{0:T(1024)(128)(4,1)}), s8[4194304]{0:T(1024)(128)(4,1)S(1)}, s32[]{:S(2)}) async-start(s8[6291456]{0:T(1024)(128)(4,1)} %bitcast.30), calls=%async_computation.2 | async-start | bytes 8388608
  4.7 58.7 %slice-start.1 = ((s8[6291456]{0:T(1024)(128)(4,1)}), s8[2097152]{0:T(1024)(128)(4,1)S(1)}, s32[]{:S(2)}) async-start(s8[6291456]{0:T(1024)(128)(4,1)} %bitcast.30), calls=%async_computation.3 | async-start | bytes 4194304
  61.5 2.0 %copy-start.1 = (bf16[8,128,2048]{2,1,0:T(8,128)(2,1)}, bf16[8,128,2048]{2,1,0:T(8,128)(2,1)S(1)}, u32[]{:S(2)}) copy-start(bf16[8,128,2048]{2,1,0:T(8,128)(2,1)S(1)} %all_to_all.24) | copy-start | bytes 12582916
  80.9 53.2 %copy-start.3 = (bf16[256,1024]{1,0:T(8,128)(2,1)S(1)}, bf16[256,1024]{1,0:T(8,128)(2,1)}, u32[]{:S(2)}) copy-start(bf16[256,1024]{1,0:T(8,128)(2,1)} %fusion.9) | copy-start | bytes 1572868

commit v9 on v6

v9 whole, which is shorter than its diff:
```python
import jax
import jax.numpy as jnp
from jax import lax
from jax.sharding import PartitionSpec as P


def slot_matrices(routes, gate_values, groups, capacity):
    tok_rows = routes.shape[0]
    row = jnp.arange(groups * capacity, dtype=jnp.int32)[:, None]
    expert_of, slot_of = row // capacity, row % capacity
    named_by = routes.T
    first = named_by[0:1, :] == expert_of
    second = named_by[1:2, :] == expert_of
    named = first | second
    order = jnp.arange(tok_rows, dtype=jnp.int32)
    later = (order[:, None] <= order[None, :]).astype(jnp.bfloat16)
    count = jnp.dot(named.astype(jnp.bfloat16), later, preferred_element_type=jnp.float32)
    hit = named & (count == (slot_of + 1).astype(jnp.float32))
    gates = gate_values.astype(jnp.float32).T
    weight = jnp.where(first, gates[0:1, :], jnp.where(second, gates[1:2, :], 0.0))
    weighted = jnp.where(hit, weight, 0.0).astype(jnp.bfloat16)
    return hit.astype(jnp.bfloat16), weighted


def local(tokens, routes, gate_values, weight_in, weight_out):
    groups = lax.axis_size("expert")
    tok_rows, width = tokens.shape
    capacity = min(tok_rows, 2 * tok_rows * routes.shape[1] // groups)
    hidden_units = weight_out.shape[1]
    picks, weighted = lax.optimization_barrier(
        slot_matrices(routes, gate_values, groups, capacity)
    )
    outgoing = jnp.dot(picks, tokens, preferred_element_type=jnp.float32).astype(jnp.bfloat16)
    rows = lax.all_to_all(outgoing, "expert", 0, 0, tiled=True)
    projected = jnp.dot(rows, weight_in[0], preferred_element_type=jnp.float32)
    hidden = (jax.nn.silu(projected[:, :hidden_units]) * projected[:, hidden_units:]).astype(
        jnp.bfloat16
    )
    expert_out = jnp.dot(hidden, weight_out[0], preferred_element_type=jnp.float32)
    returned = lax.all_to_all(expert_out.astype(jnp.bfloat16), "expert", 0, 0, tiled=True)
    mixed = lax.dot_general(
        weighted, returned, (((0,), (0,)), ((), ())), preferred_element_type=jnp.float32
    )
    return mixed.astype(jnp.bfloat16)


def solution(mesh):
    in_specs = (
        P(("dp", "expert"), None),
        P(("dp", "expert"), None),
        P(("dp", "expert"), None),
        P("expert", None, None),
        P("expert", None, None),
    )
    out_specs = P(("dp", "expert"), None)
    return jax.shard_map(local, mesh=mesh, in_specs=in_specs, out_specs=out_specs, check_vma=False)
```

time: 127 us -> 128 us (level)
  no operation moved by 1% of the time
where the time goes in v9:
time: 128 us; the launch traced here: 126 us
  blocking collectives  109 us (85%)
  matrix products  14.9 us (12%)
    all_to_all x1, blocking collectives, local(): rows = lax.all_to_all(outgoing, 'expert', 0, 0, tiled=True)  56.7 us
    all_to_all x1, blocking collectives, local(): lax.all_to_all(expert_out.astype(jnp.bfloat16), 'expert', 0, 0, tiled=True)  52.3 us
    dot_general x1, matrix products, local(): projected = jnp.dot(rows, weight_in[0], preferred_element_type=jnp.float32)  6.65 us
    dot_general x1, matrix products, local(): jnp.dot(hidden, weight_out[0], preferred_element_type=jnp.float32)  3.7 us

profile of v9, /device:TPU:38, one launch (start us, length us, event | category | flops | bytes accessed | tf_op | source)
XLA Modules:
  0.0 126.0 jit_solution(7944780622307937094)
XLA Ops:
  0.0 0.0 copy-start
  0.0 0.0 copy-start.1
  0.0 0.8 convert_bitcast_fusion
  0.9 0.8 fusion.23
  1.7 1.1 fusion.24
  2.8 0.3 fusion.8
  3.1 0.0 copy-done.1
  3.1 0.0 slice-start
  3.1 1.3 convolution_convert_fusion
  4.4 0.0 slice-start.1
  4.4 56.7 %all_to_all.24 = bf16[8,128,2048]{2,1,0:T(8,128)(2,1)S(1)} all-to-all(bf16[8,128,2048]{2,1,0:T(8,128)(2,1)S(1)} %bitcast.22), channel_id=1, replica_groups=mesh['dp'=32,'expert'=8] {'expert'}, dimensions={0} | all-to-all | bytes 8388608 | tf_op jit(solution)/shard_map/all_to_all | solution.py:34
  61.1 0.0 slice-done
  61.1 0.0 slice-done.1
  61.1 6.7 %fusion = f32[1024,1536]{1,0:T(8,128)S(1)} fusion(bf16[1024,2048]{1,0:T(8,128)(2,1)S(1)} %bitcast.24, bf16[1,2048,1536]{2,1,0:T(8,128)(2,1)S(1)} %bitcast.34), kind=kOutput, calls=%fused_computation | convolution fusion | flops 6442450944 | bytes 16777216 | tf_op jit(solution)/shard_map/dot_general | solution.py:35
  67.8 0.0 copy-done
  67.8 3.7 %convolution_convert_fusion.1 = bf16[1024,2048]{1,0:T(8,128)(2,1)S(1)} fusion(bf16[1,768,2048]{2,1,0:T(8,128)(2,1)S(1)} %copy-done, f32[1024,1536]{1,0:T(8,128)S(1)} %fusion), kind=kOutput, calls=%fused_computation.3 | convolution fusion | flops 3228041216 | bytes 13631488 | tf_op jit(solution)/shard_map/dot_general | solution.py:39
  71.5 52.3 %all_to_all.25 = bf16[8,128,2048]{2,1,0:T(8,128)(2,1)S(1)} all-to-all(bf16[8,128,2048]{2,1,0:T(8,128)(2,1)S(1)} %bitcast.25), channel_id=1, replica_groups=mesh['dp'=32,'expert'=8] {'expert'}, dimensions={0} | all-to-all | bytes 8388608 | tf_op jit(solution)/shard_map/all_to_all | solution.py:40
  123.8 2.2 %convolution_convert_fusion.2 = bf16[256,2048]{1,0:T(8,128)(2,1)} fusion(bf16[1024,256]{1,0:T(8,128)(2,1)S(1)} %fusion.8, bf16[1024,2048]{1,0:T(8,128)(2,1)S(1)} %bitcast.23), kind=kOutput, calls=%fused_computation.7 | convolution fusion | flops 1074266112 | bytes 5767168 | tf_op jit(solution)/shard_map/dot_general | solution.py:41
  (3 shorter events, 0.0 us)
Async XLA Ops:
  0.0 67.8 %copy-start = (bf16[1,768,2048]{2,1,0:T(8,128)(2,1)S(1)}, bf16[1,768,2048]{2,1,0:T(8,128)(2,1)}, u32[]{:S(2)}) copy-start(bf16[1,768,2048]{2,1,0:T(8,128)(2,1)} %param.9) | copy-start | bytes 9437188
  0.0 3.1 %copy-start.1 = (bf16[256,2048]{1,0:T(8,128)(2,1)S(1)}, bf16[256,2048]{1,0:T(8,128)(2,1)}, u32[]{:S(2)}) copy-start(bf16[256,2048]{1,0:T(8,128)(2,1)} %param.5) | copy-start | bytes 3145732
  3.1 58.0 %slice-start = ((s8[6291456]{0:T(1024)(128)(4,1)}), s8[4194304]{0:T(1024)(128)(4,1)S(1)}, s32[]{:S(2)}) async-start(s8[6291456]{0:T(1024)(128)(4,1)} %bitcast.33), calls=%async_computation.2 | async-start | bytes 8388608
  4.4 56.8 %slice-start.1 = ((s8[6291456]{0:T(1024)(128)(4,1)}), s8[2097152]{0:T(1024)(128)(4,1)S(1)}, s32[]{:S(2)}) async-start(s8[6291456]{0:T(1024)(128)(4,1)} %bitcast.33), calls=%async_computation.3 | async-start | bytes 4194304

commit v10 on v9

v10 whole, which is shorter than its diff:
```python
import functools

import jax
import jax.numpy as jnp
from jax import lax
from jax.experimental import pallas as pl
from jax.experimental.pallas import tpu as pltpu
from jax.sharding import PartitionSpec as P

INTERPRET = False


def dispatch_kernel(capacity, block, routes_ref, gates_ref, tokens_ref, out_ref, weighted_ref):
    slots, tok_rows = weighted_ref.shape
    width = tokens_ref.shape[1]
    shift = capacity.bit_length() - 1
    row = lax.broadcasted_iota(jnp.int32, (slots, tok_rows), 0)
    expert_of = lax.shift_right_logical(row, shift)
    slot_of = lax.bitwise_and(row, capacity - 1)
    routes = routes_ref[...]
    gates = gates_ref[...].astype(jnp.float32)
    first = routes[0:1, :] == expert_of
    second = routes[1:2, :] == expert_of
    named = jnp.where(first | second, 1.0, 0.0).astype(jnp.bfloat16)
    above = lax.broadcasted_iota(jnp.int32, (tok_rows, tok_rows), 0)
    below = lax.broadcasted_iota(jnp.int32, (tok_rows, tok_rows), 1)
    later = jnp.where(above <= below, 1.0, 0.0).astype(jnp.bfloat16)
    count = jnp.dot(named, later, preferred_element_type=jnp.float32)
    hit = (first | second) & (count == (slot_of + 1).astype(jnp.float32))
    weight = jnp.where(first, gates[0:1, :], jnp.where(second, gates[1:2, :], 0.0))
    weighted_ref[...] = jnp.where(hit, weight, 0.0).astype(jnp.bfloat16)
    picks = jnp.where(hit, 1.0, 0.0).astype(jnp.bfloat16)
    for k in range(width // block):
        cols = slice(k * block, (k + 1) * block)
        out_ref[:, cols] = jnp.dot(
            picks, tokens_ref[:, cols], preferred_element_type=jnp.float32
        ).astype(out_ref.dtype)


def dispatch(routes, gate_values, tokens, groups, capacity):
    tok_rows, width = tokens.shape
    slots = groups * capacity
    return pl.pallas_call(
        functools.partial(dispatch_kernel, capacity, 512),
        out_shape=(
            jax.ShapeDtypeStruct((slots, width), tokens.dtype),
            jax.ShapeDtypeStruct((slots, tok_rows), jnp.bfloat16),
        ),
        in_specs=[pl.BlockSpec(memory_space=pltpu.VMEM)] * 3,
        out_specs=(pl.BlockSpec(memory_space=pltpu.VMEM), pl.BlockSpec(memory_space=pltpu.VMEM)),
        compiler_params=pltpu.CompilerParams(vmem_limit_bytes=48 * 1024 * 1024),
        interpret=INTERPRET,
    )(routes.T, gate_values.T, tokens)


def local(tokens, routes, gate_values, weight_in, weight_out):
    groups = lax.axis_size("expert")
    tok_rows, width = tokens.shape
    capacity = min(tok_rows, 2 * tok_rows * routes.shape[1] // groups)
    assert capacity & (capacity - 1) == 0
    hidden_units = weight_out.shape[1]
    outgoing, weighted = dispatch(routes, gate_values, tokens, groups, capacity)
    rows = lax.all_to_all(outgoing, "expert", 0, 0, tiled=True)
    projected = jnp.dot(rows, weight_in[0], preferred_element_type=jnp.float32)
    hidden = (jax.nn.silu(projected[:, :hidden_units]) * projected[:, hidden_units:]).astype(
        jnp.bfloat16
    )
    expert_out = jnp.dot(hidden, weight_out[0], preferred_element_type=jnp.float32)
    returned = lax.all_to_all(expert_out.astype(jnp.bfloat16), "expert", 0, 0, tiled=True)
    mixed = lax.dot_general(
        weighted, returned, (((0,), (0,)), ((), ())), preferred_element_type=jnp.float32
    )
    return mixed.astype(jnp.bfloat16)


def solution(mesh):
    in_specs = (
        P(("dp", "expert"), None),
        P(("dp", "expert"), None),
        P(("dp", "expert"), None),
        P("expert", None, None),
        P("expert", None, None),
    )
    out_specs = P(("dp", "expert"), None)
    return jax.shard_map(local, mesh=mesh, in_specs=in_specs, out_specs=out_specs, check_vma=False)
```

time: 128 us -> 128 us (level)
  matrix products: 14.9 us -> 12.6 us
  local copies, waits for them, and re-layouts: 0.84 us -> 2.74 us
  Pallas kernels: 0 us -> 1.74 us
    unnamed x8 -> x10, local copies, waits for them, and re-layouts: 0.02 us -> 2.74 us
    dot_general x2 -> x0, matrix products: 2.34 us -> none  [the longest x1 1.26 us: local(): jnp.dot(picks, tokens, preferred_element_type=jnp.float32)]
    pallas_call x0 -> x1, Pallas kernels: none -> 1.74 us  [dispatch(): pl.pallas_call(functools.partial(dispatch_kernel, capacity, 512), out_sha...]
where the time goes in v10:
time: 128 us; the launch traced here: 126 us
  blocking collectives  109 us (85%)
  matrix products  12.6 us (10%)
  local copies, waits for them, and re-layouts  2.74 us (2%)
  Pallas kernels  1.74 us (1%)
    all_to_all x1, blocking collectives, local(): rows = lax.all_to_all(outgoing, 'expert', 0, 0, tiled=True)  56.9 us
    all_to_all x1, blocking collectives, local(): lax.all_to_all(expert_out.astype(jnp.bfloat16), 'expert', 0, 0, tiled=True)  52.3 us
    dot_general x1, matrix products, local(): projected = jnp.dot(rows, weight_in[0], preferred_element_type=jnp.float32)  6.64 us
    dot_general x1, matrix products, local(): jnp.dot(hidden, weight_out[0], preferred_element_type=jnp.float32)  3.7 us
    unnamed x10, local copies, waits for them, and re-layouts  2.74 us

profile of v10, /device:TPU:38, one launch (start us, length us, event | category | flops | bytes accessed | tf_op | source)
XLA Modules:
  0.0 126.3 jit_solution(9261677079038809727)
XLA Ops:
  0.0 0.0 copy-start
  0.0 0.0 copy-start.1
  0.0 1.4 %copy-done.1 = bf16[256,2048]{1,0:T(8,128)(2,1)S(1)} copy-done((bf16[256,2048]{1,0:T(8,128)(2,1)S(1)}, bf16[256,2048]{1,0:T(8,128)(2,1)}, u32[]{:S(2)}) %copy-start.1) | copy-done | bytes 1048600
  1.4 0.0 copy-start.2
  1.4 0.7 copy-done.2
  2.1 0.0 copy-start.3
  2.1 0.7 copy-done.3
  2.7 1.7 %shard_map.55 = (bf16[1024,2048]{1,0:T(8,128)(2,1)S(1)}, bf16[1024,256]{1,0:T(8,128)(2,1)S(1)}) custom-call(s32[2,256]{1,0:T(2,128)S(1)} %bitcast.16, bf16[2,256]{1,0:T(2,128)(2,1)S(1)} %bitcast.17, bf16[256,2048]{1,0:T(8,128)(2,1)S(1)} %copy-done.1), custom_call_target="tpu_custom_call" | custom-call | tf_op jit(solution)/shard_map/pallas_call | solution.py:43
  4.5 0.0 copy-start.4
  4.5 56.9 %all_to_all.24 = bf16[8,128,2048]{2,1,0:T(8,128)(2,1)S(1)} all-to-all(bf16[8,128,2048]{2,1,0:T(8,128)(2,1)S(1)} %bitcast.15), channel_id=1, replica_groups=mesh['dp'=32,'expert'=8] {'expert'}, dimensions={0} | all-to-all | bytes 8388608 | tf_op jit(solution)/shard_map/all_to_all | solution.py:63
  61.4 0.0 copy-done.4
  61.4 6.6 %fusion = f32[1024,1536]{1,0:T(8,128)S(1)} fusion(bf16[1024,2048]{1,0:T(8,128)(2,1)S(1)} %bitcast.19, bf16[1,2048,1536]{2,1,0:T(8,128)(2,1)S(1)} %copy-done.4), kind=kOutput, calls=%fused_computation | convolution fusion | flops 6442450944 | bytes 16777216 | tf_op jit(solution)/shard_map/dot_general | solution.py:64
  68.0 0.0 copy-done
  68.0 3.7 %convolution_convert_fusion = bf16[1024,2048]{1,0:T(8,128)(2,1)S(1)} fusion(bf16[1,768,2048]{2,1,0:T(8,128)(2,1)S(1)} %copy-done, f32[1024,1536]{1,0:T(8,128)S(1)} %fusion), kind=kOutput, calls=%fused_computation.2 | convolution fusion | flops 3228041216 | bytes 13631488 | tf_op jit(solution)/shard_map/dot_general | solution.py:68
  71.7 52.3 %all_to_all.25 = bf16[8,128,2048]{2,1,0:T(8,128)(2,1)S(1)} all-to-all(bf16[8,128,2048]{2,1,0:T(8,128)(2,1)S(1)} %bitcast.20), channel_id=1, replica_groups=mesh['dp'=32,'expert'=8] {'expert'}, dimensions={0} | all-to-all | bytes 8388608 | tf_op jit(solution)/shard_map/all_to_all | solution.py:69
  124.0 2.2 %convolution_convert_fusion.1 = bf16[256,2048]{1,0:T(8,128)(2,1)} fusion(bf16[1024,256]{1,0:T(8,128)(2,1)S(1)} %get-tuple-element.7, bf16[1024,2048]{1,0:T(8,128)(2,1)S(1)} %bitcast.18), kind=kOutput, calls=%fused_computation.6 | convolution fusion | flops 1074266112 | bytes 5767168 | tf_op jit(solution)/shard_map/dot_general | solution.py:70
Async XLA Ops:
  0.0 68.0 %copy-start = (bf16[1,768,2048]{2,1,0:T(8,128)(2,1)S(1)}, bf16[1,768,2048]{2,1,0:T(8,128)(2,1)}, u32[]{:S(2)}) copy-start(bf16[1,768,2048]{2,1,0:T(8,128)(2,1)} %param.9) | copy-start | bytes 9437188
  0.0 1.4 %copy-start.1 = (bf16[256,2048]{1,0:T(8,128)(2,1)S(1)}, bf16[256,2048]{1,0:T(8,128)(2,1)}, u32[]{:S(2)}) copy-start(bf16[256,2048]{1,0:T(8,128)(2,1)} %tokens_ref.1) | copy-start | bytes 3145732
  1.4 0.7 copy-start.2
  2.1 0.7 copy-start.3
  4.5 56.9 %copy-start.4 = (bf16[1,2048,1536]{2,1,0:T(8,128)(2,1)S(1)}, bf16[1,2048,1536]{2,1,0:T(8,128)(2,1)}, u32[]{:S(2)}) copy-start(bf16[1,2048,1536]{2,1,0:T(8,128)(2,1)} %param.8) | copy-start | bytes 18874372

commit v11 on v9

--- a/solution.py
+++ b/solution.py
@@ -27,9 +27,7 @@
     tok_rows, width = tokens.shape
     capacity = min(tok_rows, 2 * tok_rows * routes.shape[1] // groups)
     hidden_units = weight_out.shape[1]
-    picks, weighted = lax.optimization_barrier(
-        slot_matrices(routes, gate_values, groups, capacity)
-    )
+    picks, weighted = slot_matrices(routes, gate_values, groups, capacity)
     outgoing = jnp.dot(picks, tokens, preferred_element_type=jnp.float32).astype(jnp.bfloat16)
     rows = lax.all_to_all(outgoing, "expert", 0, 0, tiled=True)
     projected = jnp.dot(rows, weight_in[0], preferred_element_type=jnp.float32)

time: 128 us -> 140 us (1.094); the launches traced: 126 us -> 140 us
  waiting for transfers between devices: 0 us -> 57.1 us
  blocking collectives: 109 us -> 56.7 us
  starting transfers between devices: 0 us -> 6.28 us
  matrix products: 14.9 us -> 18.6 us
    all_to_all x0 -> x1, waiting for transfers between devices: none -> 57.1 us  [local(): lax.all_to_all(expert_out.astype(jnp.bfloat16), 'expert', 0, 0, tiled=True)]
    all_to_all x1 -> x0, blocking collectives: 52.3 us -> none  [local(): lax.all_to_all(expert_out.astype(jnp.bfloat16), 'expert', 0, 0, tiled=True)]
    all_to_all x0 -> x1, starting transfers between devices: none -> 6.28 us  [local(): lax.all_to_all(expert_out.astype(jnp.bfloat16), 'expert', 0, 0, tiled=True)]
    dot_general x1, matrix products: 2.25 us -> 4.56 us  [local(): lax.dot_general(weighted, returned, (((0,), (0,)), ((), ())), preferred_e...]
  transfers between devices with their start and end apart: 0 -> 1, of which waited for: 0 -> 1; matrix products, arithmetic and copies ran while one was open for 0% -> 0% of each run, Pallas kernels for 0% -> 0%
where the time goes in v11:
time: 140 us
  waiting for transfers between devices  57.1 us (41%)
  blocking collectives  56.7 us (40%)
  matrix products  18.6 us (13%)
  starting transfers between devices  6.28 us (4%)
    all_to_all x1, waiting for transfers between devices, local(): lax.all_to_all(expert_out.astype(jnp.bfloat16), 'expert', 0, 0, tiled=True)  57.1 us
    all_to_all x1, blocking collectives, local(): rows = lax.all_to_all(outgoing, 'expert', 0, 0, tiled=True)  56.7 us
    dot_general x1, matrix products, local(): projected = jnp.dot(rows, weight_in[0], preferred_element_type=jnp.float32)  6.65 us
    all_to_all x1, starting transfers between devices, local(): lax.all_to_all(expert_out.astype(jnp.bfloat16), 'expert', 0, 0, tiled=True)  6.28 us
    dot_general x1, matrix products, local(): jnp.dot(hidden, weight_out[0], preferred_element_type=jnp.float32)  5.09 us
    dot_general x1, matrix products, local(): lax.dot_general(weighted, returned, (((0,), (0,)), ((), ())), preferred_e...  4.56 us
  transfers between devices with their start and end apart: 1, of which 1 were waited for; matrix products, arithmetic and copies ran while one was open for 0% of the time, Pallas kernels for 0%

profile of v11, /device:TPU:38, one launch (start us, length us, event | category | flops | bytes accessed | tf_op | source)
XLA Modules:
  0.0 139.6 jit_solution(4351464283422039198)
XLA Ops:
  0.0 0.0 copy-start
  0.0 0.0 copy-start.1
  0.0 0.9 fusion.31
  0.9 1.0 fusion.6
  1.9 0.0 copy-done.1
  1.9 0.0 slice-start
  1.9 1.3 convolution_convert_fusion
  3.2 0.0 slice-start.1
  3.2 56.7 %all_to_all.24 = bf16[8,128,2048]{2,1,0:T(8,128)(2,1)S(1)} all-to-all(bf16[8,128,2048]{2,1,0:T(8,128)(2,1)S(1)} %bitcast.21), channel_id=1, replica_groups=mesh['dp'=32,'expert'=8] {'expert'}, dimensions={0} | all-to-all | bytes 8388608 | tf_op jit(solution)/shard_map/all_to_all | solution.py:32
  59.9 0.0 slice-done
  60.0 0.0 slice-done.1
  60.0 6.7 %fusion = f32[1024,1536]{1,0:T(8,128)S(1)} fusion(bf16[1024,2048]{1,0:T(8,128)(2,1)S(1)} %bitcast.23, bf16[1,2048,1536]{2,1,0:T(8,128)(2,1)S(1)} %bitcast.32), kind=kOutput, calls=%fused_computation | convolution fusion | flops 6442450944 | bytes 16777216 | tf_op jit(solution)/shard_map/dot_general | solution.py:33
  66.6 0.0 copy-done
  66.6 5.1 %convolution_convert_fusion.1 = bf16[1024,2048]{1,0:T(8,128)(2,1)} fusion(bf16[1,768,2048]{2,1,0:T(8,128)(2,1)S(1)} %copy-done, f32[1024,1536]{1,0:T(8,128)S(1)} %fusion), kind=kOutput, calls=%fused_computation.3 | convolution fusion | flops 3228041216 | bytes 13631488 | tf_op jit(solution)/shard_map/dot_general | solution.py:37
  71.7 0.0 copy-start.2
  71.7 6.3 %all-to-all-start.1 = ((bf16[8,128,2048]{2,1,0:T(8,128)(2,1)}), bf16[8,128,2048]{2,1,0:T(8,128)(2,1)}, u32[]{:S(2)}, u32[]{:S(2)}) async-start(bf16[8,128,2048]{2,1,0:T(8,128)(2,1)} %bitcast.22), calls=%async_computation.1 | async-start | bytes 8388608 | tf_op jit(solution)/shard_map/all_to_all | solution.py:38
  78.0 0.0 copy-done.2
  78.0 57.1 %all-to-all-done.1 = bf16[8,128,2048]{2,1,0:T(8,128)(2,1)} async-done(((bf16[8,128,2048]{2,1,0:T(8,128)(2,1)}), bf16[8,128,2048]{2,1,0:T(8,128)(2,1)}, u32[]{:S(2)}, u32[]{:S(2)}) %all-to-all-start.1) | async-done | bytes 4194336 | tf_op jit(solution)/shard_map/all_to_all | solution.py:38
  135.1 4.6 %convolution_convert_fusion.2 = bf16[256,2048]{1,0:T(8,128)(2,1)} fusion(bf16[1024,2048]{1,0:T(8,128)(2,1)} %bitcast.11, pred[1024,256]{1,0:T(32,128)(4,1)S(1)} %fusion.6, f32[256]{0:T(256)S(1)} %bitcast.30, f32[256]{0:T(256)S(1)} %bitcast.29, s32[256]{0:T(256)S(1)} %bitcast.28, s32[256]{0:T(256)S(1)} %bitcast.26, s32[1024]{0:T(1024)S(1)} %get-tuple-element.9), kind=kOutput, calls=%fused_computation.7 | convolution fusion | flops 1075576832 | bytes 5513216 | tf_op jit(solution)/shard_map/dot_general | solution.py:39
  (4 shorter events, 0.0 us)
Async XLA Ops:
  0.0 66.6 %copy-start = (bf16[1,768,2048]{2,1,0:T(8,128)(2,1)S(1)}, bf16[1,768,2048]{2,1,0:T(8,128)(2,1)}, u32[]{:S(2)}) copy-start(bf16[1,768,2048]{2,1,0:T(8,128)(2,1)} %param.9) | copy-start | bytes 9437188
  0.0 1.9 %copy-start.1 = (bf16[256,2048]{1,0:T(8,128)(2,1)S(1)}, bf16[256,2048]{1,0:T(8,128)(2,1)}, u32[]{:S(2)}) copy-start(bf16[256,2048]{1,0:T(8,128)(2,1)} %param.5) | copy-start | bytes 3145732
  1.9 58.0 %slice-start = ((s8[6291456]{0:T(1024)(128)(4,1)}), s8[4194304]{0:T(1024)(128)(4,1)S(1)}, s32[]{:S(2)}) async-start(s8[6291456]{0:T(1024)(128)(4,1)} %bitcast.31), calls=%async_computation.2 | async-start | bytes 8388608
  3.2 56.8 %slice-start.1 = ((s8[6291456]{0:T(1024)(128)(4,1)}), s8[2097152]{0:T(1024)(128)(4,1)S(1)}, s32[]{:S(2)}) async-start(s8[6291456]{0:T(1024)(128)(4,1)} %bitcast.31), calls=%async_computation.3 | async-start | bytes 4194304
  71.7 6.3 %copy-start.2 = (bf16[256,2]{0,1:T(2,128)(2,1)S(1)}, bf16[256,2]{0,1:T(2,128)(2,1)}, u32[]{:S(2)}) copy-start(bf16[256,2]{0,1:T(2,128)(2,1)} %param.7) | copy-start | bytes 3076
  71.7 63.4 %all-to-all-start.1 = ((bf16[8,128,2048]{2,1,0:T(8,128)(2,1)}), bf16[8,128,2048]{2,1,0:T(8,128)(2,1)}, u32[]{:S(2)}, u32[]{:S(2)}) async-start(bf16[8,128,2048]{2,1,0:T(8,128)(2,1)} %bitcast.22), calls=%async_computation.1 | async-start | bytes 8388608 | tf_op jit(solution)/shard_map/all_to_all | solution.py:38
